TPU v7x, 256 devices: a whole 4x4x8 slice. The times are simulated.
256 devices in a mesh: dp: 32 (over x_lo, z, core), blk: 8 (over y, x_hi).
Axes of the slice: x: 4 (x_hi: 2, x_lo: 2; x = x_hi * 2 + x_lo), y: 4, z: 8, core: 2. Of those that a mesh axis runs over, the one named last changes fastest.
Arguments:
- inputs: bfloat16 [8, 16384, 4096], P('blk', 'dp'), may hold values from -6 to 6
- out_grads: bfloat16 [8, 16384, 4096], P('blk', 'dp'), may hold values from -8 to 8
- test_matrix: bfloat16 [8, 4096, 256], P('blk'), may hold values from -6 to 6
- momentum: bfloat16 [8, 4096, 4096], P(None, 'blk', 'dp'), may hold values from -6 to 6
Outputs:
- update: bfloat16 [8, 4096, 4096], P(None, 'blk', 'dp')
All inputs are finite; a program needn't handle non-finite values.
Results may differ from a plain program's by a relative error of at most 0.0035.
Values may be sent and summed in bfloat16 or wider, within the bound.
No kernel may reach another device: no remote copies, remote signals or barrier semaphores. Data moves between devices by JAX's collectives and lax.ppermute only.
A program may use at most 128 MiB of HBM per device.

v0:
```python
import functools
import jax
import jax.numpy as jnp
from jax import lax
from jax.sharding import Mesh
from jax.sharding import PartitionSpec as P
from jax.experimental import pallas as pl
from jax.experimental.pallas import tpu as pltpu

DP = ("dp_0", "dp_1", "dp_2")


def filled_up(lines, devices):
    spare = -len(lines) % devices
    return jnp.pad(lines, [(0, spare)] + [(0, 0)] * (lines.ndim - 1))


def copy_for_each(x, axis):
    devices = lax.axis_size(axis)
    return lax.all_to_all(jnp.broadcast_to(x[None], (devices, *x.shape)), axis, 0, 0, tiled=True)


def in_order(blocks, dim):
    blocks = jnp.moveaxis(blocks, 0, dim)
    lengths = blocks.shape
    return blocks.reshape(*lengths[:dim], lengths[dim] * lengths[dim + 1], *lengths[dim + 2 :])


def whole_of(x, axes, dim):
    far, near = axes
    first = copy_for_each(x, far)
    blocks = jnp.swapaxes(copy_for_each(first, near), 0, 1)
    return in_order(blocks.reshape(-1, *x.shape), dim)


def in_blocks(x, dim, devices):
    lengths = x.shape
    blocks = x.reshape(*lengths[:dim], devices, lengths[dim] // devices, *lengths[dim + 1 :])
    return jnp.moveaxis(blocks, dim, 0)


def sum_at_owner(x, axis, dim):
    blocks = in_blocks(x, dim, lax.axis_size(axis))
    arrived = lax.all_to_all(blocks, axis, split_axis=0, concat_axis=0, tiled=True)
    return arrived.sum(axis=0)


def sum_by_axis(x, axes, dim):
    far, near = axes
    blocks = in_blocks(x, dim, lax.axis_size(far))
    nearer = sum_at_owner(blocks, near, dim + 1).astype(jnp.bfloat16)
    arrived = lax.all_to_all(nearer, far, split_axis=0, concat_axis=0, tiled=True)
    return arrived.astype(jnp.float32).sum(axis=0)


def total_of(x, axes):
    lines = x.reshape(-1, x.shape[-1])
    padded = filled_up(lines, lax.axis_size(axes[0]) * lax.axis_size(axes[1]))
    whole = whole_of(sum_by_axis(padded, axes, 0).astype(jnp.bfloat16), axes, 0)
    return lax.slice_in_dim(whole, 0, len(lines)).reshape(x.shape)


def chip_first_sum(x, far, near):
    halves = x.reshape(lax.axis_size(near), -1, x.shape[-1])
    nearer = lax.all_to_all(halves, near, split_axis=0, concat_axis=0, tiled=True).sum(axis=0)
    blocks = in_blocks(nearer, 0, lax.axis_size(far)).astype(jnp.bfloat16)
    arrived = lax.all_to_all(blocks, far, split_axis=0, concat_axis=0, tiled=True)
    own = arrived.astype(jnp.float32).sum(axis=0).astype(jnp.bfloat16)
    first = copy_for_each(own, far)
    return in_order(copy_for_each(first, near).reshape(-1, *own.shape), 0)


def collect(x, axis, dim):
    blocks = copy_for_each(x, axis)
    return in_order(blocks, dim)


def total_of_2(x, axes):
    lines = x.reshape(-1, x.shape[-1])
    own = sum_at_owner(filled_up(lines, lax.axis_size(axes)), axes, 0)
    whole = collect(own, axes, 0)
    return whole[: len(lines)].reshape(x.shape)


def butterfly_sum(x, axes, masks):
    size = 1
    for a in axes:
        size *= lax.axis_size(a)
    for m in masks:
        x = x + lax.ppermute(x, axes, [(i, i ^ m) for i in range(size)])
    return x


def shifted(x, axis, s):
    n = lax.axis_size(axis)
    return lax.ppermute(x, axis, [(j, (j + s) % n) for j in range(n)])


def spread(stack, axis):
    n = lax.axis_size(axis)
    me = lax.axis_index(axis)
    mine = jnp.roll(stack, -me, axis=0)
    pieces = [mine[0]] + [shifted(mine[s], axis, s) for s in range(1, n)]
    ordered = jnp.stack([pieces[(-i) % n] for i in range(n)])
    return jnp.roll(ordered, me, axis=0)


def gather_all(x, axis):
    n = lax.axis_size(axis)
    me = lax.axis_index(axis)
    pieces = [x] + [shifted(x, axis, s) for s in range(1, n)]
    ordered = jnp.stack([pieces[(-i) % n] for i in range(n)])
    return jnp.roll(ordered, me, axis=0)


def ring_sum(x, axis):
    n = lax.axis_size(axis)
    parts = x.reshape(n, x.shape[0] // n, *x.shape[1:])
    own = lax.all_to_all(parts, axis, 0, 0, tiled=True).sum(axis=0)
    return collect(own, axis, 0)


def inner_gram(columns):
    return lax.dot_general(
        columns, columns, (((0,), (0,)), ((), ())), precision=lax.Precision.HIGHEST
    )


def mm(a, b):
    return jnp.dot(a, b, precision=lax.Precision.HIGHEST)


def _factor_kernel(a_ref, w_ref, r_ref, panel_rows):
    n = a_ref.shape[0]
    rows_i = lax.broadcasted_iota(jnp.int32, (n, n), 0)
    cols_i = lax.broadcasted_iota(jnp.int32, (n, n), 1)
    r_ref[:, :n] = a_ref[...]
    r_ref[:, n:] = jnp.where(rows_i == cols_i, 1.0, 0.0).astype(jnp.float32)
    sub = lax.broadcasted_iota(jnp.int32, (panel_rows, 1), 0)
    lane_wide = lax.broadcasted_iota(jnp.int32, (1, 2 * n), 1)
    for p in range(n // panel_rows):
        r0 = panel_rows * p
        panel = r_ref[r0:r0 + panel_rows, :]
        for r in range(panel_rows):
            j = r0 + r
            part = panel[:, (j // 128) * 128:(j // 128 + 1) * 128]
            column = part[:, j % 128:j % 128 + 1]
            inv = lax.rsqrt(column[r:r + 1, :])
            row = jnp.where(lane_wide < j, 0.0, panel[r:r + 1, :] * inv)
            mult = jnp.where(sub > r, column * inv, 0.0)
            panel = jnp.where(sub == r, row, panel - mult * row)
        r_ref[r0:r0 + panel_rows, :] = panel
        low = r0 + panel_rows
        if low < n:
            outer = lax.dot_general(
                panel[:, :n], panel, (((0,), (0,)), ((), ())),
                precision=lax.Precision.HIGHEST, preferred_element_type=jnp.float32,
            )
            r_ref[low:, :] = r_ref[low:, :] - outer[low:, :]
    w_ref[...] = r_ref[:, n:]


def inverse_factor(matrix):
    n = matrix.shape[0]
    sym = (matrix + matrix.T) * 0.5
    return pl.pallas_call(
        functools.partial(_factor_kernel, panel_rows=64),
        out_shape=jax.ShapeDtypeStruct((n, n), jnp.float32),
        scratch_shapes=[pltpu.VMEM((n, 2 * n), jnp.float32)],
    )(sym)


def cholesky_pass(columns, gram_matrix):
    return mm(columns, inverse_factor(gram_matrix).T)


def shards(inputs, out_grads, test_matrix, momentum):
    features = inputs[0]
    errors = out_grads[0]
    probes = test_matrix[0]
    replicas = lax.axis_size(DP)
    scale = 1.0 / (features.shape[1] * features.shape[0] * replicas)
    projected = jnp.dot(features, probes, preferred_element_type=jnp.float32).astype(jnp.bfloat16)
    token_gram = lax.dot_general(
        errors, errors, (((1,), (1,)), ((), ())), preferred_element_type=jnp.float32
    ).astype(jnp.bfloat16)
    mixed_rows = jnp.dot(token_gram, projected, preferred_element_type=jnp.float32).astype(
        jnp.bfloat16
    )
    sketch_term = (
        lax.dot_general(
            features, mixed_rows, (((0,), (0,)), ((), ())), preferred_element_type=jnp.float32
        )
        * scale
    )
    sketch = chip_first_sum(sketch_term, ("dp_0", "dp_1"), "dp_2").astype(jnp.float32)
    basis = cholesky_pass(sketch, inner_gram(sketch)).astype(jnp.bfloat16)
    reduced = jnp.dot(features, basis, preferred_element_type=jnp.float32).astype(jnp.bfloat16)
    shaped = jnp.dot(token_gram, reduced, preferred_element_type=jnp.float32).astype(jnp.bfloat16)
    core_term = (
        lax.dot_general(
            reduced, shaped, (((0,), (0,)), ((), ())), preferred_element_type=jnp.float32
        )
        * scale
    )
    core_matrix = ring_sum(butterfly_sum(core_term, DP, (1, 16)), "dp_1")
    shifted = core_matrix + jnp.eye(core_matrix.shape[0], dtype=jnp.float32)
    inverse = inverse_factor(shifted)
    factor = mm(inverse.T, mm(inverse, core_matrix))
    blocks = spread(momentum, "blk")
    columns = blocks.reshape(-1, blocks.shape[-1])
    coeffs = lax.dot_general(
        basis, columns, (((0,), (0,)), ((), ())), preferred_element_type=jnp.float32
    )
    scaled = jnp.dot(factor, coeffs, precision=lax.Precision.HIGHEST).astype(jnp.bfloat16)
    fresh = (
        columns.astype(jnp.float32) - jnp.dot(basis, scaled, preferred_element_type=jnp.float32)
    ).astype(jnp.bfloat16)
    return spread(fresh.reshape(blocks.shape), "blk")


def solution(mesh):
    torus = Mesh(mesh.devices.reshape(2, 8, 2, mesh.shape["blk"]), ("dp_0", "dp_1", "dp_2", "blk"))
    in_specs = (P("blk", DP, None), P("blk", DP, None), P("blk", None, None), P(None, "blk", DP))
    out_specs = P(None, "blk", DP)
    return jax.shard_map(
        shards, mesh=torus, in_specs=in_specs, out_specs=out_specs, check_vma=False
    )
```

profile of v0, /device:TPU:8, one launch (start us, length us, event | category | flops | bytes accessed | tf_op | source)
XLA Modules:
  0.0 255.9 jit_solution(1757201083374775705)
XLA Ops:
  0.0 6.0 %fusion.9 = bf16[512,512]{1,0:T(8,128)(2,1)S(1)} fusion(bf16[1,512,4096]{2,1,0:T(8,128)(2,1)} %param.7), kind=kOutput, calls=%fused_computation.21 | convolution fusion | flops 2147745792 | bytes 4718592 | tf_op jit(solution)/shard_map/dot_general | solution.py:184
  6.0 1.3 fusion.12
  7.3 5.9 %convolution_multiply_fusion = f32[256,4096]{1,0:T(8,128)} fusion(bf16[1,512,4096]{2,1,0:T(8,128)(2,1)} %param.6, bf16[512,512]{1,0:T(8,128)(2,1)S(1)} %fusion.9, bf16[512,256]{1,0:T(8,128)(2,1)S(1)} %fusion.12), kind=kOutput, calls=%fused_computation | convolution fusion | flops 1209139200 | bytes 9175040 | tf_op jit(solution)/shard_map/dot_general | solution.py:191
  13.2 2.5 copy.35
  15.6 8.1 %all_to_all.30 = f32[2,2048,256]{1,2,0:T(8,128)} all-to-all(f32[2,2048,256]{1,2,0:T(8,128)S(1)} %bitcast.128), channel_id=1, replica_groups=mesh['dp_0'=2,'dp_1'=8,'dp_2'=2,'blk'=8] {'dp_2'}, dimensions={0} | all-to-all | bytes 8388608 | tf_op jit(solution)/shard_map/all_to_all | solution.py:65
  23.8 2.7 %reduce_sum.30 = bf16[2048,256]{0,1:T(8,128)(2,1)S(1)} reduce(f32[2,2048,256]{1,2,0:T(8,128)} %all_to_all.30, f32[]{:T(128)} %constant.27.clone.1), dimensions={0}, to_apply=%region_0.2 | reduce | flops 524288 | bytes 5242884 | tf_op jit(solution)/shard_map/reduce_sum | solution.py:65
  26.7 36.3 %all_to_all.31 = bf16[16,128,256]{1,2,0:T(8,128)(2,1)S(1)} all-to-all(bf16[16,128,256]{1,2,0:T(8,128)(2,1)S(1)} %copy_bitcast_fusion.1), channel_id=1, replica_groups=mesh['dp_0'=2,'dp_1'=8,'dp_2'=2,'blk'=8] {'dp_0','dp_1'}, dimensions={0} | all-to-all | bytes 2097152 | tf_op jit(solution)/shard_map/all_to_all | solution.py:67
  64.3 4.8 %all-to-all-start.2 = ((bf16[16,128,256]{2,1,0:T(8,128)(2,1)}), bf16[16,128,256]{2,1,0:T(8,128)(2,1)S(1)}, u32[]{:S(2)}, u32[]{:S(2)}) async-start(bf16[16,128,256]{2,1,0:T(8,128)(2,1)} %broadcast_in_dim.6), calls=%async_computation.2 | async-start | bytes 2097152 | tf_op jit(solution)/shard_map/all_to_all | solution.py:20
  69.1 1.6 fusion.25
  71.6 2.6 %collective-permute-start = (bf16[512,128]{1,0:T(8,128)(2,1)}, bf16[512,128]{1,0:T(8,128)(2,1)}, u32[]{:S(2)}, u32[]{:S(2)}) collective-permute-start(bf16[512,128]{1,0:T(8,128)(2,1)} %get-tuple-element.20), channel_id=1, source_target_pairs={{0,7},{1,0},{2,1},{3,2},{4,3},{5,4},{6,5},{7,6},{8,15},{9,8},{10,9... | collective-permute-start | bytes 393224 | tf_op jit(solution)/shard_map/ppermute | solution.py:96
  74.2 3.1 %collective-permute-start.1 = (bf16[512,128]{1,0:T(8,128)(2,1)}, bf16[512,128]{1,0:T(8,128)(2,1)}, u32[]{:S(2)}, u32[]{:S(2)}) collective-permute-start(bf16[512,128]{1,0:T(8,128)(2,1)} %get-tuple-element.19), channel_id=1, source_target_pairs={{0,6},{1,7},{2,0},{3,1},{4,2},{5,3},{6,4},{7,5},{8,14},{9,15},{10,... | collective-permute-start | bytes 393224 | tf_op jit(solution)/shard_map/ppermute | solution.py:96
  78.6 3.7 %collective-permute-start.4 = (bf16[512,128]{1,0:T(8,128)(2,1)S(1)}, bf16[512,128]{1,0:T(8,128)(2,1)}, u32[]{:S(2)}, u32[]{:S(2)}) collective-permute-start(bf16[512,128]{1,0:T(8,128)(2,1)S(1)} %get-tuple-element.16), channel_id=1, source_target_pairs={{0,3},{1,4},{2,5},{3,6},{4,7},{5,0},{6,1},{7,2},{8,11},{9,12},{10,... | collective-permute-start | bytes 393224 | tf_op jit(solution)/shard_map/ppermute | solution.py:96
  82.3 14.0 %all-to-all-done.2 = bf16[16,128,256]{2,1,0:T(8,128)(2,1)S(1)} async-done(((bf16[16,128,256]{2,1,0:T(8,128)(2,1)}), bf16[16,128,256]{2,1,0:T(8,128)(2,1)S(1)}, u32[]{:S(2)}, u32[]{:S(2)}) %all-to-all-start.2) | async-done | bytes 1048608 | tf_op jit(solution)/shard_map/all_to_all | solution.py:20
  96.5 5.4 %all_to_all.32 = bf16[2,16,128,256]{3,2,1,0:T(8,128)(2,1)S(1)} all-to-all(bf16[2,16,128,256]{3,2,1,0:T(8,128)(2,1)S(1)} %broadcast_in_dim.7), channel_id=1, replica_groups=mesh['dp_0'=2,'dp_1'=8,'dp_2'=2,'blk'=8] {'dp_2'}, dimensions={0} | all-to-all | bytes 4194304 | tf_op jit(solution)/shard_map/all_to_all | solution.py:20
  101.9 1.3 copy-done.1
  104.9 25.0 %shard_map.46 = f32[256,256]{1,0:T(8,128)} custom-call(f32[256,256]{1,0:T(8,128)} %fusion.27.a_ref), custom_call_target="tpu_custom_call" | custom-call | tf_op jit(solution)/shard_map/pallas_call | solution.py:166
  129.9 3.6 %convolution_convert_fusion = bf16[4096,256]{1,0:T(8,128)(2,1)S(1)} fusion(bf16[4096,256]{1,0:T(8,128)(2,1)} %bitcast.126, f32[256,256]{1,0:T(8,128)} %shard_map.46), kind=kOutput, calls=%fused_computation.1 | convolution fusion | flops 3222274048 | bytes 4456448 | tf_op jit(solution)/shard_map/dot_general | solution.py:130
  133.5 1.3 copy-done.2
  134.8 12.5 %fusion.17 = bf16[256,512]{1,0:T(8,128)(2,1)S(1)} fusion(bf16[4096,256]{1,0:T(8,128)(2,1)S(1)} %convolution_convert_fusion, bf16[1,512,4096]{2,1,0:T(8,128)(2,1)S(1)} %copy-done.5), kind=kOutput, calls=%fused_computation.23 | convolution fusion | flops 1073872896 | bytes 6553600 | tf_op jit(solution)/shard_map/dot_general | solution.py:198
  148.2 1.6 bitcast_dynamic-update-slice_fusion.13
  149.7 1.6 collective-permute-start.5
  151.3 1.6 bitcast_dynamic-update-slice_fusion.12
  152.9 2.7 %collective-permute-start.6 = (bf16[512,128]{1,0:T(8,128)(2,1)S(1)}, bf16[512,128]{1,0:T(8,128)(2,1)S(1)}, u32[]{:S(2)}, u32[]{:S(2)}) collective-permute-start(bf16[512,128]{1,0:T(8,128)(2,1)S(1)} %get-tuple-element.14), channel_id=1, source_target_pairs={{0,1},{1,2},{2,3},{3,4},{4,5},{5,6},{6,7},{7,0},{8,9},{9,10},{10,1... | collective-permute-start | bytes 393224 | tf_op jit(solution)/shard_map/ppermute | solution.py:96
  155.8 1.6 bitcast_dynamic-update-slice_fusion.11
  157.3 1.6 bitcast_dynamic-update-slice_fusion.10
  158.9 5.8 %collective-permute-done.8 = f32[256,256]{1,0:T(8,128)S(1)} collective-permute-done((f32[256,256]{1,0:T(8,128)S(1)}, f32[256,256]{1,0:T(8,128)S(1)}, u32[]{:S(2)}, u32[]{:S(2)}) %collective-permute-start.8) | collective-permute-done | bytes 262176 | tf_op jit(solution)/shard_map/ppermute | solution.py:90
  165.4 4.3 %all-to-all-start.4 = ((f32[8,32,256]{2,1,0:T(8,128)}), f32[8,32,256]{2,1,0:T(8,128)S(1)}, u32[]{:S(2)}, u32[]{:S(2)}) async-start(f32[8,32,256]{2,1,0:T(8,128)} %bitcast.24), calls=%async_computation.4 | async-start | bytes 524288 | tf_op jit(solution)/shard_map/all_to_all | solution.py:119
  169.7 1.6 bitcast_dynamic-update-slice_fusion.9
  172.0 9.1 %all-to-all-done.4 = f32[8,32,256]{2,1,0:T(8,128)S(1)} async-done(((f32[8,32,256]{2,1,0:T(8,128)}), f32[8,32,256]{2,1,0:T(8,128)S(1)}, u32[]{:S(2)}, u32[]{:S(2)}) %all-to-all-start.4) | async-done | bytes 262176 | tf_op jit(solution)/shard_map/all_to_all | solution.py:119
  181.8 3.4 %all-to-all-start.5 = ((f32[8,32,256]{2,1,0:T(8,128)}), f32[8,32,256]{2,1,0:T(8,128)S(1)}, u32[]{:S(2)}, u32[]{:S(2)}) async-start(f32[8,32,256]{2,1,0:T(8,128)} %broadcast_in_dim.8), calls=%async_computation.5 | async-start | bytes 524288 | tf_op jit(solution)/shard_map/all_to_all | solution.py:20
  185.9 1.6 fusion.24
  188.2 7.3 %all-to-all-done.5 = f32[8,32,256]{2,1,0:T(8,128)S(1)} async-done(((f32[8,32,256]{2,1,0:T(8,128)}), f32[8,32,256]{2,1,0:T(8,128)S(1)}, u32[]{:S(2)}, u32[]{:S(2)}) %all-to-all-start.5) | async-done | bytes 262176 | tf_op jit(solution)/shard_map/all_to_all | solution.py:20
  196.4 1.7 convert_add_fusion
  198.1 1.8 copy.26
  199.9 1.8 fusion.26.a_ref
  201.7 25.0 %shard_map.47 = f32[256,256]{1,0:T(8,128)} custom-call(f32[256,256]{1,0:T(8,128)} %fusion.26.a_ref), custom_call_target="tpu_custom_call" | custom-call | tf_op jit(solution)/shard_map/pallas_call | solution.py:166
  226.7 1.3 fusion.28
  228.0 1.5 fusion.29
  230.0 2.3 fusion
  233.0 3.0 %collective-permute-start.9 = (bf16[512,128]{1,0:T(8,128)(2,1)S(1)}, bf16[512,128]{1,0:T(8,128)(2,1)S(1)}, u32[]{:S(2)}, u32[]{:S(2)}) collective-permute-start(bf16[512,128]{1,0:T(8,128)(2,1)S(1)} %get-tuple-element.12), channel_id=1, source_target_pairs={{0,7},{1,0},{2,1},{3,2},{4,3},{5,4},{6,5},{7,6},{8,15},{9,8},{10,9... | collective-permute-start | bytes 393224 | tf_op jit(solution)/shard_map/ppermute | solution.py:96
  235.9 1.7 collective-permute-start.10
  238.8 1.2 collective-permute-start.12
  240.0 3.7 %collective-permute-start.13 = (bf16[512,128]{1,0:T(8,128)(2,1)S(1)}, bf16[512,128]{1,0:T(8,128)(2,1)S(1)}, u32[]{:S(2)}, u32[]{:S(2)}) collective-permute-start(bf16[512,128]{1,0:T(8,128)(2,1)S(1)} %get-tuple-element.8), channel_id=1, source_target_pairs={{0,3},{1,4},{2,5},{3,6},{4,7},{5,0},{6,1},{7,2},{8,11},{9,12},{10,... | collective-permute-start | bytes 393224 | tf_op jit(solution)/shard_map/ppermute | solution.py:96
  244.7 2.3 collective-permute-done.10
  247.0 1.8 collective-permute-done.13
  248.9 1.2 collective-permute-done.14
  250.1 4.2 %collective-permute-done.15 = bf16[512,128]{1,0:T(8,128)(2,1)S(1)} collective-permute-done((bf16[512,128]{1,0:T(8,128)(2,1)S(1)}, bf16[512,128]{1,0:T(8,128)(2,1)S(1)}, u32[]{:S(2)}, u32[]{:S(2)}) %collective-permute-start.15) | collective-permute-done | bytes 131104 | tf_op jit(solution)/shard_map/ppermute | solution.py:96
  254.3 1.4 fusion.22
  (60 shorter events, 14.2 us)
Async XLA Ops:
  0.0 6.0 %copy-start = (bf16[1,4096,256]{2,1,0:T(8,128)(2,1)S(1)}, bf16[1,4096,256]{2,1,0:T(8,128)(2,1)}, u32[]{:S(2)}) copy-start(bf16[1,4096,256]{2,1,0:T(8,128)(2,1)} %param.8) | copy-start | bytes 6291460
  0.0 6.0 %copy-start.4 = (bf16[1,512,4096]{2,1,0:T(8,128)(2,1)S(1)}, bf16[1,512,4096]{2,1,0:T(8,128)(2,1)}, u32[]{:S(2)}) copy-start(bf16[1,512,4096]{2,1,0:T(8,128)(2,1)} %param.6) | copy-start | bytes 12582916
  6.0 1.3 copy-start.6
  64.3 31.9 %all-to-all-start.2 = ((bf16[16,128,256]{2,1,0:T(8,128)(2,1)}), bf16[16,128,256]{2,1,0:T(8,128)(2,1)S(1)}, u32[]{:S(2)}, u32[]{:S(2)}) async-start(bf16[16,128,256]{2,1,0:T(8,128)(2,1)} %broadcast_in_dim.6), calls=%async_computation.2 | async-start | bytes 2097152 | tf_op jit(solution)/shard_map/all_to_all | solution.py:20
  71.6 76.4 %collective-permute-start = (bf16[512,128]{1,0:T(8,128)(2,1)}, bf16[512,128]{1,0:T(8,128)(2,1)}, u32[]{:S(2)}, u32[]{:S(2)}) collective-permute-start(bf16[512,128]{1,0:T(8,128)(2,1)} %get-tuple-element.20), channel_id=1, source_target_pairs={{0,7},{1,0},{2,1},{3,2},{4,3},{5,4},{6,5},{7,6},{8,15},{9,8},{10,9... | collective-permute-start | bytes 393224 | tf_op jit(solution)/shard_map/ppermute | solution.py:96
  74.2 75.5 %collective-permute-start.1 = (bf16[512,128]{1,0:T(8,128)(2,1)}, bf16[512,128]{1,0:T(8,128)(2,1)}, u32[]{:S(2)}, u32[]{:S(2)}) collective-permute-start(bf16[512,128]{1,0:T(8,128)(2,1)} %get-tuple-element.19), channel_id=1, source_target_pairs={{0,6},{1,7},{2,0},{3,1},{4,2},{5,3},{6,4},{7,5},{8,14},{9,15},{10,... | collective-permute-start | bytes 393224 | tf_op jit(solution)/shard_map/ppermute | solution.py:96
  77.3 78.4 %collective-permute-start.2 = (bf16[512,128]{1,0:T(8,128)(2,1)}, bf16[512,128]{1,0:T(8,128)(2,1)}, u32[]{:S(2)}, u32[]{:S(2)}) collective-permute-start(bf16[512,128]{1,0:T(8,128)(2,1)} %get-tuple-element.18), channel_id=1, source_target_pairs={{0,5},{1,6},{2,7},{3,0},{4,1},{5,2},{6,3},{7,4},{8,13},{9,14},{10,... | collective-permute-start | bytes 393224 | tf_op jit(solution)/shard_map/ppermute | solution.py:96
  77.6 79.7 %collective-permute-start.3 = (bf16[512,128]{1,0:T(8,128)(2,1)}, bf16[512,128]{1,0:T(8,128)(2,1)}, u32[]{:S(2)}, u32[]{:S(2)}) collective-permute-start(bf16[512,128]{1,0:T(8,128)(2,1)} %get-tuple-element.17), channel_id=1, source_target_pairs={{0,4},{1,5},{2,6},{3,7},{4,0},{5,1},{6,2},{7,3},{8,12},{9,13},{10,... | collective-permute-start | bytes 393224 | tf_op jit(solution)/shard_map/ppermute | solution.py:96
  78.6 91.2 %collective-permute-start.4 = (bf16[512,128]{1,0:T(8,128)(2,1)S(1)}, bf16[512,128]{1,0:T(8,128)(2,1)}, u32[]{:S(2)}, u32[]{:S(2)}) collective-permute-start(bf16[512,128]{1,0:T(8,128)(2,1)S(1)} %get-tuple-element.16), channel_id=1, source_target_pairs={{0,3},{1,4},{2,5},{3,6},{4,7},{5,0},{6,1},{7,2},{8,11},{9,12},{10,... | collective-permute-start | bytes 393224 | tf_op jit(solution)/shard_map/ppermute | solution.py:96
  101.9 1.3 copy-start.1
  129.9 4.9 %copy-start.5 = (bf16[1,512,4096]{2,1,0:T(8,128)(2,1)S(1)}, bf16[1,512,4096]{2,1,0:T(8,128)(2,1)}, u32[]{:S(2)}) copy-start(bf16[1,512,4096]{2,1,0:T(8,128)(2,1)} %param.6) | copy-start | bytes 12582916
  133.5 1.3 copy-start.2
  134.8 12.5 %copy-start.7 = (bf16[512,512]{1,0:T(8,128)(2,1)S(1)}, bf16[512,512]{1,0:T(8,128)(2,1)}, u32[]{:S(2)}) copy-start(bf16[512,512]{1,0:T(8,128)(2,1)} %copy-done.6) | copy-start | bytes 1572868
  147.9 4.9 %collective-permute-start.7 = (f32[256,256]{1,0:T(8,128)S(1)}, f32[256,256]{1,0:T(8,128)S(1)}, u32[]{:S(2)}, u32[]{:S(2)}) collective-permute-start(f32[256,256]{1,0:T(8,128)S(1)} %fusion.21), channel_id=1, source_target_pairs={{0,8},{8,0},{16,24},{24,16},{32,40},{40,32},{48,56},{56,48},{64,72... | collective-permute-start | bytes 786440 | tf_op jit(solution)/shard_map/ppermute | solution.py:90
  149.7 21.6 %collective-permute-start.5 = (bf16[512,128]{1,0:T(8,128)(2,1)S(1)}, bf16[512,128]{1,0:T(8,128)(2,1)S(1)}, u32[]{:S(2)}, u32[]{:S(2)}) collective-permute-start(bf16[512,128]{1,0:T(8,128)(2,1)S(1)} %get-tuple-element.15), channel_id=1, source_target_pairs={{0,2},{1,3},{2,4},{3,5},{4,6},{5,7},{6,0},{7,1},{8,10},{9,11},{10,... | collective-permute-start | bytes 393224 | tf_op jit(solution)/shard_map/ppermute | solution.py:96
  152.9 32.3 %collective-permute-start.6 = (bf16[512,128]{1,0:T(8,128)(2,1)S(1)}, bf16[512,128]{1,0:T(8,128)(2,1)S(1)}, u32[]{:S(2)}, u32[]{:S(2)}) collective-permute-start(bf16[512,128]{1,0:T(8,128)(2,1)S(1)} %get-tuple-element.14), channel_id=1, source_target_pairs={{0,1},{1,2},{2,3},{3,4},{4,5},{5,6},{6,7},{7,0},{8,9},{9,10},{10,1... | collective-permute-start | bytes 393224 | tf_op jit(solution)/shard_map/ppermute | solution.py:96
  155.7 9.0 %collective-permute-start.8 = (f32[256,256]{1,0:T(8,128)S(1)}, f32[256,256]{1,0:T(8,128)S(1)}, u32[]{:S(2)}, u32[]{:S(2)}) collective-permute-start(f32[256,256]{1,0:T(8,128)S(1)} %add.24), channel_id=1, source_target_pairs={{0,128},{8,136},{16,144},{24,152},{32,160},{40,168},{48,176},{56,1... | collective-permute-start | bytes 786440 | tf_op jit(solution)/shard_map/ppermute | solution.py:90
  165.4 15.6 %all-to-all-start.4 = ((f32[8,32,256]{2,1,0:T(8,128)}), f32[8,32,256]{2,1,0:T(8,128)S(1)}, u32[]{:S(2)}, u32[]{:S(2)}) async-start(f32[8,32,256]{2,1,0:T(8,128)} %bitcast.24), calls=%async_computation.4 | async-start | bytes 524288 | tf_op jit(solution)/shard_map/all_to_all | solution.py:119
  181.8 13.8 %all-to-all-start.5 = ((f32[8,32,256]{2,1,0:T(8,128)}), f32[8,32,256]{2,1,0:T(8,128)S(1)}, u32[]{:S(2)}, u32[]{:S(2)}) async-start(f32[8,32,256]{2,1,0:T(8,128)} %broadcast_in_dim.8), calls=%async_computation.5 | async-start | bytes 524288 | tf_op jit(solution)/shard_map/all_to_all | solution.py:20
  185.2 2.3 copy-start.3
  233.0 10.8 %collective-permute-start.9 = (bf16[512,128]{1,0:T(8,128)(2,1)S(1)}, bf16[512,128]{1,0:T(8,128)(2,1)S(1)}, u32[]{:S(2)}, u32[]{:S(2)}) collective-permute-start(bf16[512,128]{1,0:T(8,128)(2,1)S(1)} %get-tuple-element.12), channel_id=1, source_target_pairs={{0,7},{1,0},{2,1},{3,2},{4,3},{5,4},{6,5},{7,6},{8,15},{9,8},{10,9... | collective-permute-start | bytes 393224 | tf_op jit(solution)/shard_map/ppermute | solution.py:96
  235.9 11.0 %collective-permute-start.10 = (bf16[512,128]{1,0:T(8,128)(2,1)S(1)}, bf16[512,128]{1,0:T(8,128)(2,1)S(1)}, u32[]{:S(2)}, u32[]{:S(2)}) collective-permute-start(bf16[512,128]{1,0:T(8,128)(2,1)S(1)} %get-tuple-element.11), channel_id=1, source_target_pairs={{0,6},{1,7},{2,0},{3,1},{4,2},{5,3},{6,4},{7,5},{8,14},{9,15},{10,... | collective-permute-start | bytes 393224 | tf_op jit(solution)/shard_map/ppermute | solution.py:96
  237.6 9.4 %collective-permute-start.11 = (bf16[512,128]{1,0:T(8,128)(2,1)S(1)}, bf16[512,128]{1,0:T(8,128)(2,1)S(1)}, u32[]{:S(2)}, u32[]{:S(2)}) collective-permute-start(bf16[512,128]{1,0:T(8,128)(2,1)S(1)} %get-tuple-element.10), channel_id=1, source_target_pairs={{0,5},{1,6},{2,7},{3,0},{4,1},{5,2},{6,3},{7,4},{8,13},{9,14},{10,... | collective-permute-start | bytes 393224 | tf_op jit(solution)/shard_map/ppermute | solution.py:96
  238.8 8.3 %collective-permute-start.12 = (bf16[512,128]{1,0:T(8,128)(2,1)S(1)}, bf16[512,128]{1,0:T(8,128)(2,1)S(1)}, u32[]{:S(2)}, u32[]{:S(2)}) collective-permute-start(bf16[512,128]{1,0:T(8,128)(2,1)S(1)} %get-tuple-element.9), channel_id=1, source_target_pairs={{0,4},{1,5},{2,6},{3,7},{4,0},{5,1},{6,2},{7,3},{8,12},{9,13},{10,... | collective-permute-start | bytes 393224 | tf_op jit(solution)/shard_map/ppermute | solution.py:96
  240.0 8.9 %collective-permute-start.13 = (bf16[512,128]{1,0:T(8,128)(2,1)S(1)}, bf16[512,128]{1,0:T(8,128)(2,1)S(1)}, u32[]{:S(2)}, u32[]{:S(2)}) collective-permute-start(bf16[512,128]{1,0:T(8,128)(2,1)S(1)} %get-tuple-element.8), channel_id=1, source_target_pairs={{0,3},{1,4},{2,5},{3,6},{4,7},{5,0},{6,1},{7,2},{8,11},{9,12},{10,... | collective-permute-start | bytes 393224 | tf_op jit(solution)/shard_map/ppermute | solution.py:96
  243.7 6.4 %collective-permute-start.14 = (bf16[512,128]{1,0:T(8,128)(2,1)S(1)}, bf16[512,128]{1,0:T(8,128)(2,1)S(1)}, u32[]{:S(2)}, u32[]{:S(2)}) collective-permute-start(bf16[512,128]{1,0:T(8,128)(2,1)S(1)} %get-tuple-element.7), channel_id=1, source_target_pairs={{0,2},{1,3},{2,4},{3,5},{4,6},{5,7},{6,0},{7,1},{8,10},{9,11},{10,... | collective-permute-start | bytes 393224 | tf_op jit(solution)/shard_map/ppermute | solution.py:96
  246.9 7.4 %collective-permute-start.15 = (bf16[512,128]{1,0:T(8,128)(2,1)S(1)}, bf16[512,128]{1,0:T(8,128)(2,1)S(1)}, u32[]{:S(2)}, u32[]{:S(2)}) collective-permute-start(bf16[512,128]{1,0:T(8,128)(2,1)S(1)} %get-tuple-element.6), channel_id=1, source_target_pairs={{0,1},{1,2},{2,3},{3,4},{4,5},{5,6},{6,7},{7,0},{8,9},{9,10},{10,1... | collective-permute-start | bytes 393224 | tf_op jit(solution)/shard_map/ppermute | solution.py:96
where the time goes:
time: 259 us; the launch traced here: 256 us
  Pallas kernels  50.1 us (19%)
  blocking collectives  49.8 us (19%)
  waiting for transfers between devices  45.7 us (18%)
  starting transfers between devices  39.6 us (15%)
  matrix products  36.8 us (14%)
  local copies, waits for them, and re-layouts  20.4 us (8%)
  other arithmetic  12.9 us (5%)
    pallas_call x2, Pallas kernels, inverse_factor(): pl.pallas_call(functools.partial(_factor_kernel, panel_rows=64), out_shap...  50.1 us
    all_to_all x1, blocking collectives, chip_first_sum(): lax.all_to_all(blocks, far, split_axis=0, concat_axis=0, tiled=True)  36.3 us
    ppermute x14, starting transfers between devices, shifted(): return lax.ppermute(x, axis, [(j, (j + s) % n) for j in range(n)])  26.7 us
    all_to_all x2, waiting for transfers between devices, copy_for_each(): lax.all_to_all(jnp.broadcast_to(x[None], (devices, *x.shape)), axis, 0, 0...  21.3 us
    dot_general x1, matrix products, shards(): jnp.dot(features, basis, preferred_element_type=jnp.float32)  12.5 us
    unnamed x28, local copies, waits for them, and re-layouts  11.2 us
    ppermute x14, waiting for transfers between devices, shifted(): return lax.ppermute(x, axis, [(j, (j + s) % n) for j in range(n)])  9.51 us
    all_to_all x1, waiting for transfers between devices, ring_sum(): own = lax.all_to_all(parts, axis, 0, 0, tiled=True).sum(axis=0)  9.05 us
  transfers between devices with their start and end apart: 19, of which 8 were waited for; matrix products, arithmetic and copies ran while one was open for 13% of the time, Pallas kernels for 10%

commit v1 on v0

--- a/solution.py
+++ b/solution.py
@@ -63,8 +63,12 @@
 def chip_first_sum(x, far, near):
     halves = x.reshape(lax.axis_size(near), -1, x.shape[-1])
     nearer = lax.all_to_all(halves, near, split_axis=0, concat_axis=0, tiled=True).sum(axis=0)
-    blocks = in_blocks(nearer, 0, lax.axis_size(far)).astype(jnp.bfloat16)
-    arrived = lax.all_to_all(blocks, far, split_axis=0, concat_axis=0, tiled=True)
+    outer_axis, inner_axis = far
+    blocks = nearer.reshape(lax.axis_size(outer_axis), -1, *nearer.shape[1:])
+    crossed = lax.all_to_all(blocks.astype(jnp.bfloat16), outer_axis, 0, 0, tiled=True)
+    partial = crossed.astype(jnp.float32).sum(axis=0)
+    parts = partial.reshape(lax.axis_size(inner_axis), -1, *partial.shape[1:])
+    arrived = lax.all_to_all(parts.astype(jnp.bfloat16), inner_axis, 0, 0, tiled=True)
     own = arrived.astype(jnp.float32).sum(axis=0).astype(jnp.bfloat16)
     first = copy_for_each(own, far)
     return in_order(copy_for_each(first, near).reshape(-1, *own.shape), 0)

time: 259 us -> 263 us (1.015)
  blocking collectives: 49.8 us -> 55.3 us
  waiting for transfers between devices: 45.7 us -> 42.3 us
    all_to_all x1 -> x2, blocking collectives: 36.3 us -> 41.7 us  [the longest x1 25.1 us: chip_first_sum(): lax.all_to_all(parts.astype(jnp.bfloat16), inner_axis, 0, 0, tiled=True)]
    all_to_all x2, waiting for transfers between devices: 21.3 us -> 18.5 us  [copy_for_each(): lax.all_to_all(jnp.broadcast_to(x[None], (devices, *x.shape)), axis, 0, 0...]
where the time goes in v1:
time: 263 us; the launch traced here: 260 us
  blocking collectives  55.3 us (21%)
  Pallas kernels  50.1 us (19%)
  waiting for transfers between devices  42.3 us (16%)
  starting transfers between devices  39.2 us (15%)
  matrix products  36.8 us (14%)
  local copies, waits for them, and re-layouts  21.5 us (8%)
  other arithmetic  14 us (5%)
    pallas_call x2, Pallas kernels, inverse_factor(): pl.pallas_call(functools.partial(_factor_kernel, panel_rows=64), out_shap...  50.1 us
    ppermute x14, starting transfers between devices, shifted(): return lax.ppermute(x, axis, [(j, (j + s) % n) for j in range(n)])  27.2 us
    all_to_all x1, blocking collectives, chip_first_sum(): lax.all_to_all(parts.astype(jnp.bfloat16), inner_axis, 0, 0, tiled=True)  25.1 us
    all_to_all x2, waiting for transfers between devices, copy_for_each(): lax.all_to_all(jnp.broadcast_to(x[None], (devices, *x.shape)), axis, 0, 0...  18.5 us
    all_to_all x1, blocking collectives, chip_first_sum(): lax.all_to_all(blocks.astype(jnp.bfloat16), outer_axis, 0, 0, tiled=True)  16.6 us
    dot_general x1, matrix products, shards(): jnp.dot(features, basis, preferred_element_type=jnp.float32)  12.5 us
    unnamed x28, local copies, waits for them, and re-layouts  11.3 us
    ppermute x14, waiting for transfers between devices, shifted(): return lax.ppermute(x, axis, [(j, (j + s) % n) for j in range(n)])  9.43 us
  transfers between devices with their start and end apart: 19, of which 8 were waited for; matrix products, arithmetic and copies ran while one was open for 13% of the time, Pallas kernels for 10%

profile of v1, /device:TPU:8, one launch (start us, length us, event | category | flops | bytes accessed | tf_op | source)
XLA Modules:
  0.0 259.9 jit_solution(18011219146820373619)
XLA Ops:
  0.0 6.0 %fusion.9 = bf16[512,512]{1,0:T(8,128)(2,1)S(1)} fusion(bf16[1,512,4096]{2,1,0:T(8,128)(2,1)} %param.7), kind=kOutput, calls=%fused_computation.21 | convolution fusion | flops 2147745792 | bytes 4718592 | tf_op jit(solution)/shard_map/dot_general | solution.py:188
  6.0 1.3 fusion.12
  7.3 5.9 %convolution_multiply_fusion = f32[256,4096]{1,0:T(8,128)} fusion(bf16[1,512,4096]{2,1,0:T(8,128)(2,1)} %param.6, bf16[512,512]{1,0:T(8,128)(2,1)S(1)} %fusion.9, bf16[512,256]{1,0:T(8,128)(2,1)S(1)} %fusion.12), kind=kOutput, calls=%fused_computation | convolution fusion | flops 1209139200 | bytes 9175040 | tf_op jit(solution)/shard_map/dot_general | solution.py:195
  13.2 2.5 copy.48
  15.6 8.2 %all_to_all.35 = f32[2,2048,256]{1,2,0:T(8,128)} all-to-all(f32[2,2048,256]{1,2,0:T(8,128)S(1)} %bitcast.130), channel_id=1, replica_groups=mesh['dp_0'=2,'dp_1'=8,'dp_2'=2,'blk'=8] {'dp_2'}, dimensions={0} | all-to-all | bytes 8388608 | tf_op jit(solution)/shard_map/all_to_all | solution.py:65
  23.8 2.7 %reduce_sum.42 = bf16[2048,256]{0,1:T(8,128)(2,1)S(1)} reduce(f32[2,2048,256]{1,2,0:T(8,128)} %all_to_all.35, f32[]{:T(128)} %constant.28.clone.1), dimensions={0}, to_apply=%region_0.2 | reduce | flops 524288 | bytes 5242884 | tf_op jit(solution)/shard_map/reduce_sum | solution.py:65
  26.5 16.6 %all_to_all.36 = bf16[2,1024,256]{1,2,0:T(8,128)(2,1)S(1)} all-to-all(bf16[2,1024,256]{1,2,0:T(8,128)(2,1)S(1)} %bitcast.133), channel_id=1, replica_groups=mesh['dp_0'=2,'dp_1'=8,'dp_2'=2,'blk'=8] {'dp_0'}, dimensions={0} | all-to-all | bytes 2097152 | tf_op jit(solution)/shard_map/all_to_all | solution.py:68
  45.4 25.1 %all_to_all.37 = bf16[8,128,256]{1,2,0:T(8,128)(2,1)S(1)} all-to-all(bf16[8,128,256]{1,2,0:T(8,128)(2,1)S(1)} %copy_bitcast_fusion.2), channel_id=1, replica_groups=mesh['dp_0'=2,'dp_1'=8,'dp_2'=2,'blk'=8] {'dp_1'}, dimensions={0} | all-to-all | bytes 1048576 | tf_op jit(solution)/shard_map/all_to_all | solution.py:71
  71.8 3.7 %all-to-all-start.3 = ((bf16[16,128,256]{2,1,0:T(8,128)(2,1)}), bf16[16,128,256]{2,1,0:T(8,128)(2,1)S(1)}, u32[]{:S(2)}, u32[]{:S(2)}) async-start(bf16[16,128,256]{2,1,0:T(8,128)(2,1)} %broadcast_in_dim.6), calls=%async_computation.3 | async-start | bytes 2097152 | tf_op jit(solution)/shard_map/all_to_all | solution.py:20
  75.5 1.6 fusion.25
  78.0 3.0 %collective-permute-start = (bf16[512,128]{1,0:T(8,128)(2,1)}, bf16[512,128]{1,0:T(8,128)(2,1)}, u32[]{:S(2)}, u32[]{:S(2)}) collective-permute-start(bf16[512,128]{1,0:T(8,128)(2,1)} %get-tuple-element.20), channel_id=1, source_target_pairs={{0,7},{1,0},{2,1},{3,2},{4,3},{5,4},{6,5},{7,6},{8,15},{9,8},{10,9... | collective-permute-start | bytes 393224 | tf_op jit(solution)/shard_map/ppermute | solution.py:100
  81.0 3.1 %collective-permute-start.1 = (bf16[512,128]{1,0:T(8,128)(2,1)}, bf16[512,128]{1,0:T(8,128)(2,1)}, u32[]{:S(2)}, u32[]{:S(2)}) collective-permute-start(bf16[512,128]{1,0:T(8,128)(2,1)} %get-tuple-element.19), channel_id=1, source_target_pairs={{0,6},{1,7},{2,0},{3,1},{4,2},{5,3},{6,4},{7,5},{8,14},{9,15},{10,... | collective-permute-start | bytes 393224 | tf_op jit(solution)/shard_map/ppermute | solution.py:100
  84.9 4.1 %collective-permute-start.4 = (bf16[512,128]{1,0:T(8,128)(2,1)S(1)}, bf16[512,128]{1,0:T(8,128)(2,1)}, u32[]{:S(2)}, u32[]{:S(2)}) collective-permute-start(bf16[512,128]{1,0:T(8,128)(2,1)S(1)} %get-tuple-element.16), channel_id=1, source_target_pairs={{0,3},{1,4},{2,5},{3,6},{4,7},{5,0},{6,1},{7,2},{8,11},{9,12},{10,... | collective-permute-start | bytes 393224 | tf_op jit(solution)/shard_map/ppermute | solution.py:100
  89.1 11.1 %all-to-all-done.3 = bf16[16,128,256]{2,1,0:T(8,128)(2,1)S(1)} async-done(((bf16[16,128,256]{2,1,0:T(8,128)(2,1)}), bf16[16,128,256]{2,1,0:T(8,128)(2,1)S(1)}, u32[]{:S(2)}, u32[]{:S(2)}) %all-to-all-start.3) | async-done | bytes 1048608 | tf_op jit(solution)/shard_map/all_to_all | solution.py:20
  100.4 5.4 %all_to_all.38 = bf16[2,16,128,256]{3,2,1,0:T(8,128)(2,1)S(1)} all-to-all(bf16[2,16,128,256]{3,2,1,0:T(8,128)(2,1)S(1)} %broadcast_in_dim.7), channel_id=1, replica_groups=mesh['dp_0'=2,'dp_1'=8,'dp_2'=2,'blk'=8] {'dp_2'}, dimensions={0} | all-to-all | bytes 4194304 | tf_op jit(solution)/shard_map/all_to_all | solution.py:20
  105.9 1.3 copy-done.1
  108.8 25.0 %shard_map.46 = f32[256,256]{1,0:T(8,128)} custom-call(f32[256,256]{1,0:T(8,128)} %fusion.27.a_ref), custom_call_target="tpu_custom_call" | custom-call | tf_op jit(solution)/shard_map/pallas_call | solution.py:170
  133.9 3.6 %convolution_convert_fusion = bf16[4096,256]{1,0:T(8,128)(2,1)S(1)} fusion(bf16[4096,256]{1,0:T(8,128)(2,1)} %bitcast.128, f32[256,256]{1,0:T(8,128)} %shard_map.46), kind=kOutput, calls=%fused_computation.1 | convolution fusion | flops 3222274048 | bytes 4456448 | tf_op jit(solution)/shard_map/dot_general | solution.py:134
  137.5 1.3 copy-done.2
  138.8 12.5 %fusion.17 = bf16[256,512]{1,0:T(8,128)(2,1)S(1)} fusion(bf16[4096,256]{1,0:T(8,128)(2,1)S(1)} %convolution_convert_fusion, bf16[1,512,4096]{2,1,0:T(8,128)(2,1)S(1)} %copy-done.5), kind=kOutput, calls=%fused_computation.23 | convolution fusion | flops 1073872896 | bytes 6553600 | tf_op jit(solution)/shard_map/dot_general | solution.py:202
  152.1 1.6 bitcast_dynamic-update-slice_fusion.13
  153.7 1.6 collective-permute-start.5
  155.3 1.6 bitcast_dynamic-update-slice_fusion.12
  156.9 3.3 %collective-permute-start.6 = (bf16[512,128]{1,0:T(8,128)(2,1)S(1)}, bf16[512,128]{1,0:T(8,128)(2,1)S(1)}, u32[]{:S(2)}, u32[]{:S(2)}) collective-permute-start(bf16[512,128]{1,0:T(8,128)(2,1)S(1)} %get-tuple-element.14), channel_id=1, source_target_pairs={{0,1},{1,2},{2,3},{3,4},{4,5},{5,6},{6,7},{7,0},{8,9},{9,10},{10,1... | collective-permute-start | bytes 393224 | tf_op jit(solution)/shard_map/ppermute | solution.py:100
  160.3 1.6 bitcast_dynamic-update-slice_fusion.11
  161.8 1.6 bitcast_dynamic-update-slice_fusion.10
  163.4 5.4 %collective-permute-done.8 = f32[256,256]{1,0:T(8,128)S(1)} collective-permute-done((f32[256,256]{1,0:T(8,128)S(1)}, f32[256,256]{1,0:T(8,128)S(1)}, u32[]{:S(2)}, u32[]{:S(2)}) %collective-permute-start.8) | collective-permute-done | bytes 262176 | tf_op jit(solution)/shard_map/ppermute | solution.py:94
  169.6 4.7 %all-to-all-start.5 = ((f32[8,32,256]{2,1,0:T(8,128)}), f32[8,32,256]{2,1,0:T(8,128)S(1)}, u32[]{:S(2)}, u32[]{:S(2)}) async-start(f32[8,32,256]{2,1,0:T(8,128)} %bitcast.24), calls=%async_computation.5 | async-start | bytes 524288 | tf_op jit(solution)/shard_map/all_to_all | solution.py:123
  174.2 1.6 bitcast_dynamic-update-slice_fusion.9
  176.5 9.0 %all-to-all-done.5 = f32[8,32,256]{2,1,0:T(8,128)S(1)} async-done(((f32[8,32,256]{2,1,0:T(8,128)}), f32[8,32,256]{2,1,0:T(8,128)S(1)}, u32[]{:S(2)}, u32[]{:S(2)}) %all-to-all-start.5) | async-done | bytes 262176 | tf_op jit(solution)/shard_map/all_to_all | solution.py:123
  186.3 3.4 %all-to-all-start.6 = ((f32[8,32,256]{2,1,0:T(8,128)}), f32[8,32,256]{2,1,0:T(8,128)S(1)}, u32[]{:S(2)}, u32[]{:S(2)}) async-start(f32[8,32,256]{2,1,0:T(8,128)} %broadcast_in_dim.8), calls=%async_computation.6 | async-start | bytes 524288 | tf_op jit(solution)/shard_map/all_to_all | solution.py:20
  190.4 1.6 fusion.24
  192.7 7.3 %all-to-all-done.6 = f32[8,32,256]{2,1,0:T(8,128)S(1)} async-done(((f32[8,32,256]{2,1,0:T(8,128)}), f32[8,32,256]{2,1,0:T(8,128)S(1)}, u32[]{:S(2)}, u32[]{:S(2)}) %all-to-all-start.6) | async-done | bytes 262176 | tf_op jit(solution)/shard_map/all_to_all | solution.py:20
  200.9 1.7 convert_add_fusion
  202.6 1.8 copy.36
  204.4 1.8 fusion.26.a_ref
  206.1 25.0 %shard_map.47 = f32[256,256]{1,0:T(8,128)} custom-call(f32[256,256]{1,0:T(8,128)} %fusion.26.a_ref), custom_call_target="tpu_custom_call" | custom-call | tf_op jit(solution)/shard_map/pallas_call | solution.py:170
  231.2 1.3 fusion.28
  232.5 1.5 fusion.29
  234.4 2.3 fusion
  237.4 2.5 collective-permute-start.9
  239.9 1.6 collective-permute-start.10
  241.6 1.7 collective-permute-start.11
  244.5 3.2 %collective-permute-start.13 = (bf16[512,128]{1,0:T(8,128)(2,1)S(1)}, bf16[512,128]{1,0:T(8,128)(2,1)S(1)}, u32[]{:S(2)}, u32[]{:S(2)}) collective-permute-start(bf16[512,128]{1,0:T(8,128)(2,1)S(1)} %get-tuple-element.8), channel_id=1, source_target_pairs={{0,3},{1,4},{2,5},{3,6},{4,7},{5,0},{6,1},{7,2},{8,11},{9,12},{10,... | collective-permute-start | bytes 393224 | tf_op jit(solution)/shard_map/ppermute | solution.py:100
  248.7 2.2 collective-permute-done.10
  251.0 2.3 collective-permute-done.13
  254.1 4.2 %collective-permute-done.15 = bf16[512,128]{1,0:T(8,128)(2,1)S(1)} collective-permute-done((bf16[512,128]{1,0:T(8,128)(2,1)S(1)}, bf16[512,128]{1,0:T(8,128)(2,1)S(1)}, u32[]{:S(2)}, u32[]{:S(2)}) %collective-permute-start.15) | collective-permute-done | bytes 131104 | tf_op jit(solution)/shard_map/ppermute | solution.py:100
  258.3 1.4 fusion.22
  (63 shorter events, 16.7 us)
Async XLA Ops:
  0.0 6.0 %copy-start = (bf16[1,4096,256]{2,1,0:T(8,128)(2,1)S(1)}, bf16[1,4096,256]{2,1,0:T(8,128)(2,1)}, u32[]{:S(2)}) copy-start(bf16[1,4096,256]{2,1,0:T(8,128)(2,1)} %param.8) | copy-start | bytes 6291460
  0.0 6.0 %copy-start.4 = (bf16[1,512,4096]{2,1,0:T(8,128)(2,1)S(1)}, bf16[1,512,4096]{2,1,0:T(8,128)(2,1)}, u32[]{:S(2)}) copy-start(bf16[1,512,4096]{2,1,0:T(8,128)(2,1)} %param.6) | copy-start | bytes 12582916
  6.0 1.3 copy-start.6
  71.8 28.4 %all-to-all-start.3 = ((bf16[16,128,256]{2,1,0:T(8,128)(2,1)}), bf16[16,128,256]{2,1,0:T(8,128)(2,1)S(1)}, u32[]{:S(2)}, u32[]{:S(2)}) async-start(bf16[16,128,256]{2,1,0:T(8,128)(2,1)} %broadcast_in_dim.6), calls=%async_computation.3 | async-start | bytes 2097152 | tf_op jit(solution)/shard_map/all_to_all | solution.py:20
  78.0 73.9 %collective-permute-start = (bf16[512,128]{1,0:T(8,128)(2,1)}, bf16[512,128]{1,0:T(8,128)(2,1)}, u32[]{:S(2)}, u32[]{:S(2)}) collective-permute-start(bf16[512,128]{1,0:T(8,128)(2,1)} %get-tuple-element.20), channel_id=1, source_target_pairs={{0,7},{1,0},{2,1},{3,2},{4,3},{5,4},{6,5},{7,6},{8,15},{9,8},{10,9... | collective-permute-start | bytes 393224 | tf_op jit(solution)/shard_map/ppermute | solution.py:100
  81.0 72.7 %collective-permute-start.1 = (bf16[512,128]{1,0:T(8,128)(2,1)}, bf16[512,128]{1,0:T(8,128)(2,1)}, u32[]{:S(2)}, u32[]{:S(2)}) collective-permute-start(bf16[512,128]{1,0:T(8,128)(2,1)} %get-tuple-element.19), channel_id=1, source_target_pairs={{0,6},{1,7},{2,0},{3,1},{4,2},{5,3},{6,4},{7,5},{8,14},{9,15},{10,... | collective-permute-start | bytes 393224 | tf_op jit(solution)/shard_map/ppermute | solution.py:100
  84.1 76.1 %collective-permute-start.2 = (bf16[512,128]{1,0:T(8,128)(2,1)}, bf16[512,128]{1,0:T(8,128)(2,1)}, u32[]{:S(2)}, u32[]{:S(2)}) collective-permute-start(bf16[512,128]{1,0:T(8,128)(2,1)} %get-tuple-element.18), channel_id=1, source_target_pairs={{0,5},{1,6},{2,7},{3,0},{4,1},{5,2},{6,3},{7,4},{8,13},{9,14},{10,... | collective-permute-start | bytes 393224 | tf_op jit(solution)/shard_map/ppermute | solution.py:100
  84.1 77.7 %collective-permute-start.3 = (bf16[512,128]{1,0:T(8,128)(2,1)}, bf16[512,128]{1,0:T(8,128)(2,1)}, u32[]{:S(2)}, u32[]{:S(2)}) collective-permute-start(bf16[512,128]{1,0:T(8,128)(2,1)} %get-tuple-element.17), channel_id=1, source_target_pairs={{0,4},{1,5},{2,6},{3,7},{4,0},{5,1},{6,2},{7,3},{8,12},{9,13},{10,... | collective-permute-start | bytes 393224 | tf_op jit(solution)/shard_map/ppermute | solution.py:100
  84.9 89.3 %collective-permute-start.4 = (bf16[512,128]{1,0:T(8,128)(2,1)S(1)}, bf16[512,128]{1,0:T(8,128)(2,1)}, u32[]{:S(2)}, u32[]{:S(2)}) collective-permute-start(bf16[512,128]{1,0:T(8,128)(2,1)S(1)} %get-tuple-element.16), channel_id=1, source_target_pairs={{0,3},{1,4},{2,5},{3,6},{4,7},{5,0},{6,1},{7,2},{8,11},{9,12},{10,... | collective-permute-start | bytes 393224 | tf_op jit(solution)/shard_map/ppermute | solution.py:100
  105.9 1.3 copy-start.1
  133.9 4.9 %copy-start.5 = (bf16[1,512,4096]{2,1,0:T(8,128)(2,1)S(1)}, bf16[1,512,4096]{2,1,0:T(8,128)(2,1)}, u32[]{:S(2)}) copy-start(bf16[1,512,4096]{2,1,0:T(8,128)(2,1)} %param.6) | copy-start | bytes 12582916
  137.4 1.3 copy-start.2
  138.8 12.5 %copy-start.7 = (bf16[512,512]{1,0:T(8,128)(2,1)S(1)}, bf16[512,512]{1,0:T(8,128)(2,1)}, u32[]{:S(2)}) copy-start(bf16[512,512]{1,0:T(8,128)(2,1)} %copy-done.6) | copy-start | bytes 1572868
  151.9 5.0 %collective-permute-start.7 = (f32[256,256]{1,0:T(8,128)S(1)}, f32[256,256]{1,0:T(8,128)S(1)}, u32[]{:S(2)}, u32[]{:S(2)}) collective-permute-start(f32[256,256]{1,0:T(8,128)S(1)} %fusion.21), channel_id=1, source_target_pairs={{0,8},{8,0},{16,24},{24,16},{32,40},{40,32},{48,56},{56,48},{64,72... | collective-permute-start | bytes 786440 | tf_op jit(solution)/shard_map/ppermute | solution.py:94
  153.7 22.1 %collective-permute-start.5 = (bf16[512,128]{1,0:T(8,128)(2,1)S(1)}, bf16[512,128]{1,0:T(8,128)(2,1)S(1)}, u32[]{:S(2)}, u32[]{:S(2)}) collective-permute-start(bf16[512,128]{1,0:T(8,128)(2,1)S(1)} %get-tuple-element.15), channel_id=1, source_target_pairs={{0,2},{1,3},{2,4},{3,5},{4,6},{5,7},{6,0},{7,1},{8,10},{9,11},{10,... | collective-permute-start | bytes 393224 | tf_op jit(solution)/shard_map/ppermute | solution.py:100
  156.9 32.8 %collective-permute-start.6 = (bf16[512,128]{1,0:T(8,128)(2,1)S(1)}, bf16[512,128]{1,0:T(8,128)(2,1)S(1)}, u32[]{:S(2)}, u32[]{:S(2)}) collective-permute-start(bf16[512,128]{1,0:T(8,128)(2,1)S(1)} %get-tuple-element.14), channel_id=1, source_target_pairs={{0,1},{1,2},{2,3},{3,4},{4,5},{5,6},{6,7},{7,0},{8,9},{9,10},{10,1... | collective-permute-start | bytes 393224 | tf_op jit(solution)/shard_map/ppermute | solution.py:100
  160.2 8.7 %collective-permute-start.8 = (f32[256,256]{1,0:T(8,128)S(1)}, f32[256,256]{1,0:T(8,128)S(1)}, u32[]{:S(2)}, u32[]{:S(2)}) collective-permute-start(f32[256,256]{1,0:T(8,128)S(1)} %add.24), channel_id=1, source_target_pairs={{0,128},{8,136},{16,144},{24,152},{32,160},{40,168},{48,176},{56,1... | collective-permute-start | bytes 786440 | tf_op jit(solution)/shard_map/ppermute | solution.py:94
  169.6 15.9 %all-to-all-start.5 = ((f32[8,32,256]{2,1,0:T(8,128)}), f32[8,32,256]{2,1,0:T(8,128)S(1)}, u32[]{:S(2)}, u32[]{:S(2)}) async-start(f32[8,32,256]{2,1,0:T(8,128)} %bitcast.24), calls=%async_computation.5 | async-start | bytes 524288 | tf_op jit(solution)/shard_map/all_to_all | solution.py:123
  186.3 13.8 %all-to-all-start.6 = ((f32[8,32,256]{2,1,0:T(8,128)}), f32[8,32,256]{2,1,0:T(8,128)S(1)}, u32[]{:S(2)}, u32[]{:S(2)}) async-start(f32[8,32,256]{2,1,0:T(8,128)} %broadcast_in_dim.8), calls=%async_computation.6 | async-start | bytes 524288 | tf_op jit(solution)/shard_map/all_to_all | solution.py:20
  189.7 2.3 copy-start.3
  237.4 10.3 %collective-permute-start.9 = (bf16[512,128]{1,0:T(8,128)(2,1)S(1)}, bf16[512,128]{1,0:T(8,128)(2,1)S(1)}, u32[]{:S(2)}, u32[]{:S(2)}) collective-permute-start(bf16[512,128]{1,0:T(8,128)(2,1)S(1)} %get-tuple-element.12), channel_id=1, source_target_pairs={{0,7},{1,0},{2,1},{3,2},{4,3},{5,4},{6,5},{7,6},{8,15},{9,8},{10,9... | collective-permute-start | bytes 393224 | tf_op jit(solution)/shard_map/ppermute | solution.py:100
  239.9 11.0 %collective-permute-start.10 = (bf16[512,128]{1,0:T(8,128)(2,1)S(1)}, bf16[512,128]{1,0:T(8,128)(2,1)S(1)}, u32[]{:S(2)}, u32[]{:S(2)}) collective-permute-start(bf16[512,128]{1,0:T(8,128)(2,1)S(1)} %get-tuple-element.11), channel_id=1, source_target_pairs={{0,6},{1,7},{2,0},{3,1},{4,2},{5,3},{6,4},{7,5},{8,14},{9,15},{10,... | collective-permute-start | bytes 393224 | tf_op jit(solution)/shard_map/ppermute | solution.py:100
  241.6 9.4 %collective-permute-start.11 = (bf16[512,128]{1,0:T(8,128)(2,1)S(1)}, bf16[512,128]{1,0:T(8,128)(2,1)S(1)}, u32[]{:S(2)}, u32[]{:S(2)}) collective-permute-start(bf16[512,128]{1,0:T(8,128)(2,1)S(1)} %get-tuple-element.10), channel_id=1, source_target_pairs={{0,5},{1,6},{2,7},{3,0},{4,1},{5,2},{6,3},{7,4},{8,13},{9,14},{10,... | collective-permute-start | bytes 393224 | tf_op jit(solution)/shard_map/ppermute | solution.py:100
  243.2 7.7 %collective-permute-start.12 = (bf16[512,128]{1,0:T(8,128)(2,1)S(1)}, bf16[512,128]{1,0:T(8,128)(2,1)S(1)}, u32[]{:S(2)}, u32[]{:S(2)}) collective-permute-start(bf16[512,128]{1,0:T(8,128)(2,1)S(1)} %get-tuple-element.9), channel_id=1, source_target_pairs={{0,4},{1,5},{2,6},{3,7},{4,0},{5,1},{6,2},{7,3},{8,12},{9,13},{10,... | collective-permute-start | bytes 393224 | tf_op jit(solution)/shard_map/ppermute | solution.py:100
  244.5 8.9 %collective-permute-start.13 = (bf16[512,128]{1,0:T(8,128)(2,1)S(1)}, bf16[512,128]{1,0:T(8,128)(2,1)S(1)}, u32[]{:S(2)}, u32[]{:S(2)}) collective-permute-start(bf16[512,128]{1,0:T(8,128)(2,1)S(1)} %get-tuple-element.8), channel_id=1, source_target_pairs={{0,3},{1,4},{2,5},{3,6},{4,7},{5,0},{6,1},{7,2},{8,11},{9,12},{10,... | collective-permute-start | bytes 393224 | tf_op jit(solution)/shard_map/ppermute | solution.py:100
  247.7 6.4 %collective-permute-start.14 = (bf16[512,128]{1,0:T(8,128)(2,1)S(1)}, bf16[512,128]{1,0:T(8,128)(2,1)S(1)}, u32[]{:S(2)}, u32[]{:S(2)}) collective-permute-start(bf16[512,128]{1,0:T(8,128)(2,1)S(1)} %get-tuple-element.7), channel_id=1, source_target_pairs={{0,2},{1,3},{2,4},{3,5},{4,6},{5,7},{6,0},{7,1},{8,10},{9,11},{10,... | collective-permute-start | bytes 393224 | tf_op jit(solution)/shard_map/ppermute | solution.py:100
  250.9 7.4 %collective-permute-start.15 = (bf16[512,128]{1,0:T(8,128)(2,1)S(1)}, bf16[512,128]{1,0:T(8,128)(2,1)S(1)}, u32[]{:S(2)}, u32[]{:S(2)}) collective-permute-start(bf16[512,128]{1,0:T(8,128)(2,1)S(1)} %get-tuple-element.6), channel_id=1, source_target_pairs={{0,1},{1,2},{2,3},{3,4},{4,5},{5,6},{6,7},{7,0},{8,9},{9,10},{10,1... | collective-permute-start | bytes 393224 | tf_op jit(solution)/shard_map/ppermute | solution.py:100

commit v2 on v0

--- a/solution.py
+++ b/solution.py
@@ -62,7 +62,8 @@
 
 def chip_first_sum(x, far, near):
     halves = x.reshape(lax.axis_size(near), -1, x.shape[-1])
-    nearer = lax.all_to_all(halves, near, split_axis=0, concat_axis=0, tiled=True).sum(axis=0)
+    crossed = lax.all_to_all(halves.astype(jnp.bfloat16), near, split_axis=0, concat_axis=0, tiled=True)
+    nearer = crossed.astype(jnp.float32).sum(axis=0)
     blocks = in_blocks(nearer, 0, lax.axis_size(far)).astype(jnp.bfloat16)
     arrived = lax.all_to_all(blocks, far, split_axis=0, concat_axis=0, tiled=True)
     own = arrived.astype(jnp.float32).sum(axis=0).astype(jnp.bfloat16)

time: 259 us -> 255 us (0.985)
  transfers between devices with their start and end apart: 19 -> 19, of which waited for: 8 -> 8; matrix products, arithmetic and copies ran while one was open for 13% -> 14% of each run, Pallas kernels for 10% -> 10%
where the time goes in v2:
time: 255 us; the launch traced here: 252 us
  Pallas kernels  50.1 us (20%)
  blocking collectives  48 us (19%)
  waiting for transfers between devices  45.6 us (18%)
  starting transfers between devices  39.6 us (16%)
  matrix products  36.2 us (14%)
  local copies, waits for them, and re-layouts  19.8 us (8%)
  other arithmetic  12.4 us (5%)
    pallas_call x2, Pallas kernels, inverse_factor(): pl.pallas_call(functools.partial(_factor_kernel, panel_rows=64), out_shap...  50.1 us
    all_to_all x1, blocking collectives, chip_first_sum(): lax.all_to_all(blocks, far, split_axis=0, concat_axis=0, tiled=True)  36.3 us
    ppermute x14, starting transfers between devices, shifted(): return lax.ppermute(x, axis, [(j, (j + s) % n) for j in range(n)])  26.7 us
    all_to_all x2, waiting for transfers between devices, copy_for_each(): lax.all_to_all(jnp.broadcast_to(x[None], (devices, *x.shape)), axis, 0, 0...  21.3 us
    dot_general x1, matrix products, shards(): jnp.dot(features, basis, preferred_element_type=jnp.float32)  12.5 us
    unnamed x28, local copies, waits for them, and re-layouts  11.2 us
    ppermute x14, waiting for transfers between devices, shifted(): return lax.ppermute(x, axis, [(j, (j + s) % n) for j in range(n)])  9.51 us
    all_to_all x1, waiting for transfers between devices, ring_sum(): own = lax.all_to_all(parts, axis, 0, 0, tiled=True).sum(axis=0)  9.05 us
  transfers between devices with their start and end apart: 19, of which 8 were waited for; matrix products, arithmetic and copies ran while one was open for 14% of the time, Pallas kernels for 10%

profile of v2, /device:TPU:8, one launch (start us, length us, event | category | flops | bytes accessed | tf_op | source)
XLA Modules:
  0.0 252.2 jit_solution(9380031678966619556)
XLA Ops:
  0.0 6.0 %fusion.10 = bf16[512,512]{1,0:T(8,128)(2,1)S(1)} fusion(bf16[1,512,4096]{2,1,0:T(8,128)(2,1)} %param.7), kind=kOutput, calls=%fused_computation.22 | convolution fusion | flops 2147745792 | bytes 4718592 | tf_op jit(solution)/shard_map/dot_general | solution.py:185
  6.0 1.3 fusion.13
  7.3 5.3 %fusion = bf16[256,4096]{1,0:T(8,128)(2,1)} fusion(bf16[1,512,4096]{2,1,0:T(8,128)(2,1)} %param.6, bf16[512,512]{1,0:T(8,128)(2,1)S(1)} %fusion.10, bf16[512,256]{1,0:T(8,128)(2,1)S(1)} %fusion.13), kind=kOutput, calls=%fused_computation.1 | convolution fusion | flops 1210187776 | bytes 7077888 | tf_op jit(solution)/shard_map/dot_general | solution.py:192
  12.6 1.7 copy.35
  14.3 6.3 %all_to_all.30 = bf16[2,2048,256]{1,2,0:T(8,128)(2,1)} all-to-all(bf16[2,2048,256]{1,2,0:T(8,128)(2,1)S(1)} %bitcast.127), channel_id=1, replica_groups=mesh['dp_0'=2,'dp_1'=8,'dp_2'=2,'blk'=8] {'dp_2'}, dimensions={0} | all-to-all | bytes 4194304 | tf_op jit(solution)/shard_map/all_to_all | solution.py:65
  20.6 2.1 reduce_sum.33
  23.0 36.3 %all_to_all.31 = bf16[16,128,256]{1,2,0:T(8,128)(2,1)S(1)} all-to-all(bf16[16,128,256]{1,2,0:T(8,128)(2,1)S(1)} %copy_bitcast_fusion.1), channel_id=1, replica_groups=mesh['dp_0'=2,'dp_1'=8,'dp_2'=2,'blk'=8] {'dp_0','dp_1'}, dimensions={0} | all-to-all | bytes 2097152 | tf_op jit(solution)/shard_map/all_to_all | solution.py:68
  60.6 4.8 %all-to-all-start.2 = ((bf16[16,128,256]{2,1,0:T(8,128)(2,1)}), bf16[16,128,256]{2,1,0:T(8,128)(2,1)S(1)}, u32[]{:S(2)}, u32[]{:S(2)}) async-start(bf16[16,128,256]{2,1,0:T(8,128)(2,1)} %broadcast_in_dim.6), calls=%async_computation.2 | async-start | bytes 2097152 | tf_op jit(solution)/shard_map/all_to_all | solution.py:20
  65.4 1.6 fusion.26
  67.9 2.6 %collective-permute-start = (bf16[512,128]{1,0:T(8,128)(2,1)}, bf16[512,128]{1,0:T(8,128)(2,1)}, u32[]{:S(2)}, u32[]{:S(2)}) collective-permute-start(bf16[512,128]{1,0:T(8,128)(2,1)} %get-tuple-element.20), channel_id=1, source_target_pairs={{0,7},{1,0},{2,1},{3,2},{4,3},{5,4},{6,5},{7,6},{8,15},{9,8},{10,9... | collective-permute-start | bytes 393224 | tf_op jit(solution)/shard_map/ppermute | solution.py:97
  70.5 3.1 %collective-permute-start.1 = (bf16[512,128]{1,0:T(8,128)(2,1)}, bf16[512,128]{1,0:T(8,128)(2,1)}, u32[]{:S(2)}, u32[]{:S(2)}) collective-permute-start(bf16[512,128]{1,0:T(8,128)(2,1)} %get-tuple-element.19), channel_id=1, source_target_pairs={{0,6},{1,7},{2,0},{3,1},{4,2},{5,3},{6,4},{7,5},{8,14},{9,15},{10,... | collective-permute-start | bytes 393224 | tf_op jit(solution)/shard_map/ppermute | solution.py:97
  74.9 3.7 %collective-permute-start.4 = (bf16[512,128]{1,0:T(8,128)(2,1)S(1)}, bf16[512,128]{1,0:T(8,128)(2,1)}, u32[]{:S(2)}, u32[]{:S(2)}) collective-permute-start(bf16[512,128]{1,0:T(8,128)(2,1)S(1)} %get-tuple-element.16), channel_id=1, source_target_pairs={{0,3},{1,4},{2,5},{3,6},{4,7},{5,0},{6,1},{7,2},{8,11},{9,12},{10,... | collective-permute-start | bytes 393224 | tf_op jit(solution)/shard_map/ppermute | solution.py:97
  78.6 13.9 %all-to-all-done.2 = bf16[16,128,256]{2,1,0:T(8,128)(2,1)S(1)} async-done(((bf16[16,128,256]{2,1,0:T(8,128)(2,1)}), bf16[16,128,256]{2,1,0:T(8,128)(2,1)S(1)}, u32[]{:S(2)}, u32[]{:S(2)}) %all-to-all-start.2) | async-done | bytes 1048608 | tf_op jit(solution)/shard_map/all_to_all | solution.py:20
  92.8 5.4 %all_to_all.32 = bf16[2,16,128,256]{3,2,1,0:T(8,128)(2,1)S(1)} all-to-all(bf16[2,16,128,256]{3,2,1,0:T(8,128)(2,1)S(1)} %broadcast_in_dim.7), channel_id=1, replica_groups=mesh['dp_0'=2,'dp_1'=8,'dp_2'=2,'blk'=8] {'dp_2'}, dimensions={0} | all-to-all | bytes 4194304 | tf_op jit(solution)/shard_map/all_to_all | solution.py:20
  98.2 1.3 copy-done.1
  101.2 25.0 %shard_map.46 = f32[256,256]{1,0:T(8,128)} custom-call(f32[256,256]{1,0:T(8,128)} %fusion.28.a_ref), custom_call_target="tpu_custom_call" | custom-call | tf_op jit(solution)/shard_map/pallas_call | solution.py:167
  126.2 3.6 %convolution_convert_fusion = bf16[4096,256]{1,0:T(8,128)(2,1)S(1)} fusion(bf16[4096,256]{1,0:T(8,128)(2,1)} %bitcast.124, f32[256,256]{1,0:T(8,128)} %shard_map.46), kind=kOutput, calls=%fused_computation.2 | convolution fusion | flops 3222274048 | bytes 4456448 | tf_op jit(solution)/shard_map/dot_general | solution.py:131
  129.8 1.3 copy-done.2
  131.1 12.5 %fusion.18 = bf16[256,512]{1,0:T(8,128)(2,1)S(1)} fusion(bf16[4096,256]{1,0:T(8,128)(2,1)S(1)} %convolution_convert_fusion, bf16[1,512,4096]{2,1,0:T(8,128)(2,1)S(1)} %copy-done.7), kind=kOutput, calls=%fused_computation.24 | convolution fusion | flops 1073872896 | bytes 6553600 | tf_op jit(solution)/shard_map/dot_general | solution.py:199
  144.5 1.6 bitcast_dynamic-update-slice_fusion.13
  146.0 1.6 collective-permute-start.5
  147.6 1.6 bitcast_dynamic-update-slice_fusion.12
  149.2 2.7 %collective-permute-start.6 = (bf16[512,128]{1,0:T(8,128)(2,1)S(1)}, bf16[512,128]{1,0:T(8,128)(2,1)S(1)}, u32[]{:S(2)}, u32[]{:S(2)}) collective-permute-start(bf16[512,128]{1,0:T(8,128)(2,1)S(1)} %get-tuple-element.14), channel_id=1, source_target_pairs={{0,1},{1,2},{2,3},{3,4},{4,5},{5,6},{6,7},{7,0},{8,9},{9,10},{10,1... | collective-permute-start | bytes 393224 | tf_op jit(solution)/shard_map/ppermute | solution.py:97
  152.1 1.6 bitcast_dynamic-update-slice_fusion.11
  153.6 1.6 bitcast_dynamic-update-slice_fusion.10
  155.2 5.8 %collective-permute-done.8 = f32[256,256]{1,0:T(8,128)S(1)} collective-permute-done((f32[256,256]{1,0:T(8,128)S(1)}, f32[256,256]{1,0:T(8,128)S(1)}, u32[]{:S(2)}, u32[]{:S(2)}) %collective-permute-start.8) | collective-permute-done | bytes 262176 | tf_op jit(solution)/shard_map/ppermute | solution.py:91
  161.7 4.3 %all-to-all-start.4 = ((f32[8,32,256]{2,1,0:T(8,128)}), f32[8,32,256]{2,1,0:T(8,128)S(1)}, u32[]{:S(2)}, u32[]{:S(2)}) async-start(f32[8,32,256]{2,1,0:T(8,128)} %bitcast.24), calls=%async_computation.4 | async-start | bytes 524288 | tf_op jit(solution)/shard_map/all_to_all | solution.py:120
  166.0 1.6 bitcast_dynamic-update-slice_fusion.9
  168.3 9.1 %all-to-all-done.4 = f32[8,32,256]{2,1,0:T(8,128)S(1)} async-done(((f32[8,32,256]{2,1,0:T(8,128)}), f32[8,32,256]{2,1,0:T(8,128)S(1)}, u32[]{:S(2)}, u32[]{:S(2)}) %all-to-all-start.4) | async-done | bytes 262176 | tf_op jit(solution)/shard_map/all_to_all | solution.py:120
  178.1 3.4 %all-to-all-start.5 = ((f32[8,32,256]{2,1,0:T(8,128)}), f32[8,32,256]{2,1,0:T(8,128)S(1)}, u32[]{:S(2)}, u32[]{:S(2)}) async-start(f32[8,32,256]{2,1,0:T(8,128)} %broadcast_in_dim.8), calls=%async_computation.5 | async-start | bytes 524288 | tf_op jit(solution)/shard_map/all_to_all | solution.py:20
  182.2 1.6 fusion.25
  184.5 7.3 %all-to-all-done.5 = f32[8,32,256]{2,1,0:T(8,128)S(1)} async-done(((f32[8,32,256]{2,1,0:T(8,128)}), f32[8,32,256]{2,1,0:T(8,128)S(1)}, u32[]{:S(2)}, u32[]{:S(2)}) %all-to-all-start.5) | async-done | bytes 262176 | tf_op jit(solution)/shard_map/all_to_all | solution.py:20
  192.7 1.7 convert_add_fusion
  194.4 1.8 copy.26
  196.2 1.8 fusion.27.a_ref
  198.0 25.0 %shard_map.47 = f32[256,256]{1,0:T(8,128)} custom-call(f32[256,256]{1,0:T(8,128)} %fusion.27.a_ref), custom_call_target="tpu_custom_call" | custom-call | tf_op jit(solution)/shard_map/pallas_call | solution.py:167
  223.0 1.3 fusion.29
  224.3 1.5 fusion.30
  226.3 2.3 fusion.1
  229.3 3.0 %collective-permute-start.9 = (bf16[512,128]{1,0:T(8,128)(2,1)S(1)}, bf16[512,128]{1,0:T(8,128)(2,1)S(1)}, u32[]{:S(2)}, u32[]{:S(2)}) collective-permute-start(bf16[512,128]{1,0:T(8,128)(2,1)S(1)} %get-tuple-element.12), channel_id=1, source_target_pairs={{0,7},{1,0},{2,1},{3,2},{4,3},{5,4},{6,5},{7,6},{8,15},{9,8},{10,9... | collective-permute-start | bytes 393224 | tf_op jit(solution)/shard_map/ppermute | solution.py:97
  232.2 1.7 collective-permute-start.10
  235.1 1.2 collective-permute-start.12
  236.3 3.7 %collective-permute-start.13 = (bf16[512,128]{1,0:T(8,128)(2,1)S(1)}, bf16[512,128]{1,0:T(8,128)(2,1)S(1)}, u32[]{:S(2)}, u32[]{:S(2)}) collective-permute-start(bf16[512,128]{1,0:T(8,128)(2,1)S(1)} %get-tuple-element.8), channel_id=1, source_target_pairs={{0,3},{1,4},{2,5},{3,6},{4,7},{5,0},{6,1},{7,2},{8,11},{9,12},{10,... | collective-permute-start | bytes 393224 | tf_op jit(solution)/shard_map/ppermute | solution.py:97
  241.0 2.3 collective-permute-done.10
  243.3 1.8 collective-permute-done.13
  245.2 1.2 collective-permute-done.14
  246.4 4.2 %collective-permute-done.15 = bf16[512,128]{1,0:T(8,128)(2,1)S(1)} collective-permute-done((bf16[512,128]{1,0:T(8,128)(2,1)S(1)}, bf16[512,128]{1,0:T(8,128)(2,1)S(1)}, u32[]{:S(2)}, u32[]{:S(2)}) %collective-permute-start.15) | collective-permute-done | bytes 131104 | tf_op jit(solution)/shard_map/ppermute | solution.py:97
  250.6 1.4 fusion.23
  (60 shorter events, 14.3 us)
Async XLA Ops:
  0.0 6.0 %copy-start = (bf16[1,4096,256]{2,1,0:T(8,128)(2,1)S(1)}, bf16[1,4096,256]{2,1,0:T(8,128)(2,1)}, u32[]{:S(2)}) copy-start(bf16[1,4096,256]{2,1,0:T(8,128)(2,1)} %param.8) | copy-start | bytes 6291460
  0.0 6.0 %copy-start.6 = (bf16[1,512,4096]{2,1,0:T(8,128)(2,1)S(1)}, bf16[1,512,4096]{2,1,0:T(8,128)(2,1)}, u32[]{:S(2)}) copy-start(bf16[1,512,4096]{2,1,0:T(8,128)(2,1)} %param.6) | copy-start | bytes 12582916
  6.0 1.3 copy-start.4
  60.6 31.9 %all-to-all-start.2 = ((bf16[16,128,256]{2,1,0:T(8,128)(2,1)}), bf16[16,128,256]{2,1,0:T(8,128)(2,1)S(1)}, u32[]{:S(2)}, u32[]{:S(2)}) async-start(bf16[16,128,256]{2,1,0:T(8,128)(2,1)} %broadcast_in_dim.6), calls=%async_computation.2 | async-start | bytes 2097152 | tf_op jit(solution)/shard_map/all_to_all | solution.py:20
  67.9 76.3 %collective-permute-start = (bf16[512,128]{1,0:T(8,128)(2,1)}, bf16[512,128]{1,0:T(8,128)(2,1)}, u32[]{:S(2)}, u32[]{:S(2)}) collective-permute-start(bf16[512,128]{1,0:T(8,128)(2,1)} %get-tuple-element.20), channel_id=1, source_target_pairs={{0,7},{1,0},{2,1},{3,2},{4,3},{5,4},{6,5},{7,6},{8,15},{9,8},{10,9... | collective-permute-start | bytes 393224 | tf_op jit(solution)/shard_map/ppermute | solution.py:97
  70.5 75.5 %collective-permute-start.1 = (bf16[512,128]{1,0:T(8,128)(2,1)}, bf16[512,128]{1,0:T(8,128)(2,1)}, u32[]{:S(2)}, u32[]{:S(2)}) collective-permute-start(bf16[512,128]{1,0:T(8,128)(2,1)} %get-tuple-element.19), channel_id=1, source_target_pairs={{0,6},{1,7},{2,0},{3,1},{4,2},{5,3},{6,4},{7,5},{8,14},{9,15},{10,... | collective-permute-start | bytes 393224 | tf_op jit(solution)/shard_map/ppermute | solution.py:97
  73.6 78.3 %collective-permute-start.2 = (bf16[512,128]{1,0:T(8,128)(2,1)}, bf16[512,128]{1,0:T(8,128)(2,1)}, u32[]{:S(2)}, u32[]{:S(2)}) collective-permute-start(bf16[512,128]{1,0:T(8,128)(2,1)} %get-tuple-element.18), channel_id=1, source_target_pairs={{0,5},{1,6},{2,7},{3,0},{4,1},{5,2},{6,3},{7,4},{8,13},{9,14},{10,... | collective-permute-start | bytes 393224 | tf_op jit(solution)/shard_map/ppermute | solution.py:97
  73.9 79.7 %collective-permute-start.3 = (bf16[512,128]{1,0:T(8,128)(2,1)}, bf16[512,128]{1,0:T(8,128)(2,1)}, u32[]{:S(2)}, u32[]{:S(2)}) collective-permute-start(bf16[512,128]{1,0:T(8,128)(2,1)} %get-tuple-element.17), channel_id=1, source_target_pairs={{0,4},{1,5},{2,6},{3,7},{4,0},{5,1},{6,2},{7,3},{8,12},{9,13},{10,... | collective-permute-start | bytes 393224 | tf_op jit(solution)/shard_map/ppermute | solution.py:97
  74.9 91.1 %collective-permute-start.4 = (bf16[512,128]{1,0:T(8,128)(2,1)S(1)}, bf16[512,128]{1,0:T(8,128)(2,1)}, u32[]{:S(2)}, u32[]{:S(2)}) collective-permute-start(bf16[512,128]{1,0:T(8,128)(2,1)S(1)} %get-tuple-element.16), channel_id=1, source_target_pairs={{0,3},{1,4},{2,5},{3,6},{4,7},{5,0},{6,1},{7,2},{8,11},{9,12},{10,... | collective-permute-start | bytes 393224 | tf_op jit(solution)/shard_map/ppermute | solution.py:97
  98.2 1.3 copy-start.1
  126.2 4.9 %copy-start.7 = (bf16[1,512,4096]{2,1,0:T(8,128)(2,1)S(1)}, bf16[1,512,4096]{2,1,0:T(8,128)(2,1)}, u32[]{:S(2)}) copy-start(bf16[1,512,4096]{2,1,0:T(8,128)(2,1)} %param.6) | copy-start | bytes 12582916
  129.8 1.3 copy-start.2
  131.1 12.5 %copy-start.5 = (bf16[512,512]{1,0:T(8,128)(2,1)S(1)}, bf16[512,512]{1,0:T(8,128)(2,1)}, u32[]{:S(2)}) copy-start(bf16[512,512]{1,0:T(8,128)(2,1)} %copy-done.4) | copy-start | bytes 1572868
  144.2 4.9 %collective-permute-start.7 = (f32[256,256]{1,0:T(8,128)S(1)}, f32[256,256]{1,0:T(8,128)S(1)}, u32[]{:S(2)}, u32[]{:S(2)}) collective-permute-start(f32[256,256]{1,0:T(8,128)S(1)} %fusion.22), channel_id=1, source_target_pairs={{0,8},{8,0},{16,24},{24,16},{32,40},{40,32},{48,56},{56,48},{64,72... | collective-permute-start | bytes 786440 | tf_op jit(solution)/shard_map/ppermute | solution.py:91
  146.0 21.6 %collective-permute-start.5 = (bf16[512,128]{1,0:T(8,128)(2,1)S(1)}, bf16[512,128]{1,0:T(8,128)(2,1)S(1)}, u32[]{:S(2)}, u32[]{:S(2)}) collective-permute-start(bf16[512,128]{1,0:T(8,128)(2,1)S(1)} %get-tuple-element.15), channel_id=1, source_target_pairs={{0,2},{1,3},{2,4},{3,5},{4,6},{5,7},{6,0},{7,1},{8,10},{9,11},{10,... | collective-permute-start | bytes 393224 | tf_op jit(solution)/shard_map/ppermute | solution.py:97
  149.2 32.3 %collective-permute-start.6 = (bf16[512,128]{1,0:T(8,128)(2,1)S(1)}, bf16[512,128]{1,0:T(8,128)(2,1)S(1)}, u32[]{:S(2)}, u32[]{:S(2)}) collective-permute-start(bf16[512,128]{1,0:T(8,128)(2,1)S(1)} %get-tuple-element.14), channel_id=1, source_target_pairs={{0,1},{1,2},{2,3},{3,4},{4,5},{5,6},{6,7},{7,0},{8,9},{9,10},{10,1... | collective-permute-start | bytes 393224 | tf_op jit(solution)/shard_map/ppermute | solution.py:97
  152.0 9.0 %collective-permute-start.8 = (f32[256,256]{1,0:T(8,128)S(1)}, f32[256,256]{1,0:T(8,128)S(1)}, u32[]{:S(2)}, u32[]{:S(2)}) collective-permute-start(f32[256,256]{1,0:T(8,128)S(1)} %add.24), channel_id=1, source_target_pairs={{0,128},{8,136},{16,144},{24,152},{32,160},{40,168},{48,176},{56,1... | collective-permute-start | bytes 786440 | tf_op jit(solution)/shard_map/ppermute | solution.py:91
  161.7 15.6 %all-to-all-start.4 = ((f32[8,32,256]{2,1,0:T(8,128)}), f32[8,32,256]{2,1,0:T(8,128)S(1)}, u32[]{:S(2)}, u32[]{:S(2)}) async-start(f32[8,32,256]{2,1,0:T(8,128)} %bitcast.24), calls=%async_computation.4 | async-start | bytes 524288 | tf_op jit(solution)/shard_map/all_to_all | solution.py:120
  178.1 13.8 %all-to-all-start.5 = ((f32[8,32,256]{2,1,0:T(8,128)}), f32[8,32,256]{2,1,0:T(8,128)S(1)}, u32[]{:S(2)}, u32[]{:S(2)}) async-start(f32[8,32,256]{2,1,0:T(8,128)} %broadcast_in_dim.8), calls=%async_computation.5 | async-start | bytes 524288 | tf_op jit(solution)/shard_map/all_to_all | solution.py:20
  181.5 2.3 copy-start.3
  229.3 10.8 %collective-permute-start.9 = (bf16[512,128]{1,0:T(8,128)(2,1)S(1)}, bf16[512,128]{1,0:T(8,128)(2,1)S(1)}, u32[]{:S(2)}, u32[]{:S(2)}) collective-permute-start(bf16[512,128]{1,0:T(8,128)(2,1)S(1)} %get-tuple-element.12), channel_id=1, source_target_pairs={{0,7},{1,0},{2,1},{3,2},{4,3},{5,4},{6,5},{7,6},{8,15},{9,8},{10,9... | collective-permute-start | bytes 393224 | tf_op jit(solution)/shard_map/ppermute | solution.py:97
  232.2 11.0 %collective-permute-start.10 = (bf16[512,128]{1,0:T(8,128)(2,1)S(1)}, bf16[512,128]{1,0:T(8,128)(2,1)S(1)}, u32[]{:S(2)}, u32[]{:S(2)}) collective-permute-start(bf16[512,128]{1,0:T(8,128)(2,1)S(1)} %get-tuple-element.11), channel_id=1, source_target_pairs={{0,6},{1,7},{2,0},{3,1},{4,2},{5,3},{6,4},{7,5},{8,14},{9,15},{10,... | collective-permute-start | bytes 393224 | tf_op jit(solution)/shard_map/ppermute | solution.py:97
  233.9 9.4 %collective-permute-start.11 = (bf16[512,128]{1,0:T(8,128)(2,1)S(1)}, bf16[512,128]{1,0:T(8,128)(2,1)S(1)}, u32[]{:S(2)}, u32[]{:S(2)}) collective-permute-start(bf16[512,128]{1,0:T(8,128)(2,1)S(1)} %get-tuple-element.10), channel_id=1, source_target_pairs={{0,5},{1,6},{2,7},{3,0},{4,1},{5,2},{6,3},{7,4},{8,13},{9,14},{10,... | collective-permute-start | bytes 393224 | tf_op jit(solution)/shard_map/ppermute | solution.py:97
  235.1 8.3 %collective-permute-start.12 = (bf16[512,128]{1,0:T(8,128)(2,1)S(1)}, bf16[512,128]{1,0:T(8,128)(2,1)S(1)}, u32[]{:S(2)}, u32[]{:S(2)}) collective-permute-start(bf16[512,128]{1,0:T(8,128)(2,1)S(1)} %get-tuple-element.9), channel_id=1, source_target_pairs={{0,4},{1,5},{2,6},{3,7},{4,0},{5,1},{6,2},{7,3},{8,12},{9,13},{10,... | collective-permute-start | bytes 393224 | tf_op jit(solution)/shard_map/ppermute | solution.py:97
  236.3 8.9 %collective-permute-start.13 = (bf16[512,128]{1,0:T(8,128)(2,1)S(1)}, bf16[512,128]{1,0:T(8,128)(2,1)S(1)}, u32[]{:S(2)}, u32[]{:S(2)}) collective-permute-start(bf16[512,128]{1,0:T(8,128)(2,1)S(1)} %get-tuple-element.8), channel_id=1, source_target_pairs={{0,3},{1,4},{2,5},{3,6},{4,7},{5,0},{6,1},{7,2},{8,11},{9,12},{10,... | collective-permute-start | bytes 393224 | tf_op jit(solution)/shard_map/ppermute | solution.py:97
  240.0 6.4 %collective-permute-start.14 = (bf16[512,128]{1,0:T(8,128)(2,1)S(1)}, bf16[512,128]{1,0:T(8,128)(2,1)S(1)}, u32[]{:S(2)}, u32[]{:S(2)}) collective-permute-start(bf16[512,128]{1,0:T(8,128)(2,1)S(1)} %get-tuple-element.7), channel_id=1, source_target_pairs={{0,2},{1,3},{2,4},{3,5},{4,6},{5,7},{6,0},{7,1},{8,10},{9,11},{10,... | collective-permute-start | bytes 393224 | tf_op jit(solution)/shard_map/ppermute | solution.py:97
  243.2 7.4 %collective-permute-start.15 = (bf16[512,128]{1,0:T(8,128)(2,1)S(1)}, bf16[512,128]{1,0:T(8,128)(2,1)S(1)}, u32[]{:S(2)}, u32[]{:S(2)}) collective-permute-start(bf16[512,128]{1,0:T(8,128)(2,1)S(1)} %get-tuple-element.6), channel_id=1, source_target_pairs={{0,1},{1,2},{2,3},{3,4},{4,5},{5,6},{6,7},{7,0},{8,9},{9,10},{10,1... | collective-permute-start | bytes 393224 | tf_op jit(solution)/shard_map/ppermute | solution.py:97

commit v3 on v2

--- a/solution.py
+++ b/solution.py
@@ -88,7 +88,8 @@
     for a in axes:
         size *= lax.axis_size(a)
     for m in masks:
-        x = x + lax.ppermute(x, axes, [(i, i ^ m) for i in range(size)])
+        sent = x.astype(jnp.bfloat16)
+        x = sent.astype(jnp.float32) + lax.ppermute(sent, axes, [(i, i ^ m) for i in range(size)]).astype(jnp.float32)
     return x
 
 
@@ -117,8 +118,8 @@
 def ring_sum(x, axis):
     n = lax.axis_size(axis)
     parts = x.reshape(n, x.shape[0] // n, *x.shape[1:])
-    own = lax.all_to_all(parts, axis, 0, 0, tiled=True).sum(axis=0)
-    return collect(own, axis, 0)
+    own = lax.all_to_all(parts.astype(jnp.bfloat16), axis, 0, 0, tiled=True).astype(jnp.float32).sum(axis=0)
+    return collect(own.astype(jnp.bfloat16), axis, 0).astype(jnp.float32)
 
 
 def inner_gram(columns):

time: 255 us -> 242 us (0.949)
  the two profiles are of different devices: /device:TPU:8 before, /device:TPU:2 now
where the time goes in v3:
time: 242 us; the launch traced here: 237 us
  Pallas kernels  50.1 us (21%)
  starting transfers between devices  47.8 us (20%)
  blocking collectives  47.6 us (20%)
  matrix products  37 us (15%)
  waiting for transfers between devices  22.5 us (9%)
  local copies, waits for them, and re-layouts  20.8 us (9%)
  other arithmetic  11.2 us (5%)
    pallas_call x2, Pallas kernels, inverse_factor(): pl.pallas_call(functools.partial(_factor_kernel, panel_rows=64), out_shap...  50.1 us
    all_to_all x1, blocking collectives, chip_first_sum(): lax.all_to_all(blocks, far, split_axis=0, concat_axis=0, tiled=True)  35.9 us
    ppermute x14, starting transfers between devices, shifted(): return lax.ppermute(x, axis, [(j, (j + s) % n) for j in range(n)])  31.7 us
    unnamed x26, local copies, waits for them, and re-layouts  12.2 us
    dot_general x1, matrix products, shards(): jnp.dot(features, basis, preferred_element_type=jnp.float32)  11.8 us
    all_to_all x2, starting transfers between devices, copy_for_each(): lax.all_to_all(jnp.broadcast_to(x[None], (devices, *x.shape)), axis, 0, 0...  9.02 us
    all_to_all x2, waiting for transfers between devices, copy_for_each(): lax.all_to_all(jnp.broadcast_to(x[None], (devices, *x.shape)), axis, 0, 0...  7.77 us
    dot_general x3, matrix products, mm(): return jnp.dot(a, b, precision=lax.Precision.HIGHEST)  6.35 us
  transfers between devices with their start and end apart: 19, of which 9 were waited for; matrix products, arithmetic and copies ran while one was open for 15% of the time, Pallas kernels for 11%

profile of v3, /device:TPU:2, one launch (start us, length us, event | category | flops | bytes accessed | tf_op | source)
XLA Modules:
  0.0 237.4 jit_solution(1876600304063410560)
XLA Ops:
  0.0 6.0 %fusion.10 = bf16[512,512]{1,0:T(8,128)(2,1)S(1)} fusion(bf16[1,512,4096]{2,1,0:T(8,128)(2,1)} %param.7), kind=kOutput, calls=%fused_computation.22 | convolution fusion | flops 2147745792 | bytes 4718592 | tf_op jit(solution)/shard_map/dot_general | solution.py:186
  6.0 1.3 fusion.13
  7.3 5.3 %fusion = bf16[256,4096]{1,0:T(8,128)(2,1)} fusion(bf16[1,512,4096]{2,1,0:T(8,128)(2,1)} %param.6, bf16[512,512]{1,0:T(8,128)(2,1)S(1)} %fusion.10, bf16[512,256]{1,0:T(8,128)(2,1)S(1)} %fusion.13), kind=kOutput, calls=%fused_computation.1 | convolution fusion | flops 1210187776 | bytes 7077888 | tf_op jit(solution)/shard_map/dot_general | solution.py:193
  12.6 1.7 copy.35
  14.3 6.3 %all_to_all.30 = bf16[2,2048,256]{1,2,0:T(8,128)(2,1)} all-to-all(bf16[2,2048,256]{1,2,0:T(8,128)(2,1)S(1)} %bitcast.127), channel_id=1, replica_groups=mesh['dp_0'=2,'dp_1'=8,'dp_2'=2,'blk'=8] {'dp_2'}, dimensions={0} | all-to-all | bytes 4194304 | tf_op jit(solution)/shard_map/all_to_all | solution.py:65
  20.6 2.1 reduce_sum.36
  23.0 35.9 %all_to_all.31 = bf16[16,128,256]{1,2,0:T(8,128)(2,1)S(1)} all-to-all(bf16[16,128,256]{1,2,0:T(8,128)(2,1)S(1)} %copy_bitcast_fusion.1), channel_id=1, replica_groups=mesh['dp_0'=2,'dp_1'=8,'dp_2'=2,'blk'=8] {'dp_0','dp_1'}, dimensions={0} | all-to-all | bytes 2097152 | tf_op jit(solution)/shard_map/all_to_all | solution.py:68
  60.2 5.6 %all-to-all-start.2 = ((bf16[16,128,256]{2,1,0:T(8,128)(2,1)}), bf16[16,128,256]{2,1,0:T(8,128)(2,1)S(1)}, u32[]{:S(2)}, u32[]{:S(2)}) async-start(bf16[16,128,256]{2,1,0:T(8,128)(2,1)} %broadcast_in_dim.6), calls=%async_computation.2 | async-start | bytes 2097152 | tf_op jit(solution)/shard_map/all_to_all | solution.py:20
  65.9 1.6 fusion.27
  68.4 4.6 %collective-permute-start = (bf16[512,128]{1,0:T(8,128)(2,1)}, bf16[512,128]{1,0:T(8,128)(2,1)}, u32[]{:S(2)}, u32[]{:S(2)}) collective-permute-start(bf16[512,128]{1,0:T(8,128)(2,1)} %get-tuple-element.20), channel_id=1, source_target_pairs={{0,7},{1,0},{2,1},{3,2},{4,3},{5,4},{6,5},{7,6},{8,15},{9,8},{10,9... | collective-permute-start | bytes 393224 | tf_op jit(solution)/shard_map/ppermute | solution.py:98
  73.7 1.3 collective-permute-start.2
  74.9 2.9 %collective-permute-start.3 = (bf16[512,128]{1,0:T(8,128)(2,1)}, bf16[512,128]{1,0:T(8,128)(2,1)}, u32[]{:S(2)}, u32[]{:S(2)}) collective-permute-start(bf16[512,128]{1,0:T(8,128)(2,1)} %get-tuple-element.17), channel_id=1, source_target_pairs={{0,4},{1,5},{2,6},{3,7},{4,0},{5,1},{6,2},{7,3},{8,12},{9,13},{10,... | collective-permute-start | bytes 393224 | tf_op jit(solution)/shard_map/ppermute | solution.py:98
  78.3 1.7 collective-permute-start.5
  80.0 1.6 bitcast_dynamic-update-slice_fusion.13
  81.6 4.3 %collective-permute-start.6 = (bf16[512,128]{1,0:T(8,128)(2,1)S(1)}, bf16[512,128]{1,0:T(8,128)(2,1)}, u32[]{:S(2)}, u32[]{:S(2)}) collective-permute-start(bf16[512,128]{1,0:T(8,128)(2,1)S(1)} %get-tuple-element.14), channel_id=1, source_target_pairs={{0,1},{1,2},{2,3},{3,4},{4,5},{5,6},{6,7},{7,0},{8,9},{9,10},{10,1... | collective-permute-start | bytes 393224 | tf_op jit(solution)/shard_map/ppermute | solution.py:98
  85.9 1.6 bitcast_dynamic-update-slice_fusion.12
  87.4 1.6 bitcast_dynamic-update-slice_fusion.11
  89.0 1.6 bitcast_dynamic-update-slice_fusion.10
  91.9 5.4 %all_to_all.32 = bf16[2,16,128,256]{3,2,1,0:T(8,128)(2,1)S(1)} all-to-all(bf16[2,16,128,256]{3,2,1,0:T(8,128)(2,1)S(1)} %broadcast_in_dim.7), channel_id=1, replica_groups=mesh['dp_0'=2,'dp_1'=8,'dp_2'=2,'blk'=8] {'dp_2'}, dimensions={0} | all-to-all | bytes 4194304 | tf_op jit(solution)/shard_map/all_to_all | solution.py:20
  97.4 1.3 copy-done.1
  100.3 25.0 %shard_map.46 = f32[256,256]{1,0:T(8,128)} custom-call(f32[256,256]{1,0:T(8,128)} %fusion.29.a_ref), custom_call_target="tpu_custom_call" | custom-call | tf_op jit(solution)/shard_map/pallas_call | solution.py:168
  125.3 3.6 %convolution_convert_fusion = bf16[4096,256]{1,0:T(8,128)(2,1)S(1)} fusion(bf16[4096,256]{1,0:T(8,128)(2,1)} %bitcast.124, f32[256,256]{1,0:T(8,128)} %shard_map.46), kind=kOutput, calls=%fused_computation.2 | convolution fusion | flops 3222274048 | bytes 4456448 | tf_op jit(solution)/shard_map/dot_general | solution.py:132
  128.9 1.3 copy-done.2
  130.3 11.8 %fusion.18 = bf16[256,512]{1,0:T(8,128)(2,1)S(1)} fusion(bf16[4096,256]{1,0:T(8,128)(2,1)S(1)} %convolution_convert_fusion, bf16[1,512,4096]{2,1,0:T(8,128)(2,1)S(1)} %copy-done.4), kind=kOutput, calls=%fused_computation.24 | convolution fusion | flops 1073872896 | bytes 6553600 | tf_op jit(solution)/shard_map/dot_general | solution.py:200
  142.9 1.6 bitcast_dynamic-update-slice_fusion.9
  144.5 1.5 collective-permute-start.8
  146.1 1.6 bitcast_dynamic-update-slice_fusion.8
  147.6 2.8 %collective-permute-done.8 = bf16[256,256]{1,0:T(8,128)(2,1)S(1)} collective-permute-done((bf16[256,256]{1,0:T(8,128)(2,1)S(1)}, bf16[256,256]{1,0:T(8,128)(2,1)S(1)}, u32[]{:S(2)}, u32[]{:S(2)}) %collective-permute-start.8) | collective-permute-done | bytes 131104 | tf_op jit(solution)/shard_map/ppermute | solution.py:92
  151.1 5.3 %all-to-all-start.4 = ((bf16[8,32,256]{2,1,0:T(8,128)(2,1)}), bf16[8,32,256]{2,1,0:T(8,128)(2,1)S(1)}, u32[]{:S(2)}, u32[]{:S(2)}) async-start(bf16[8,32,256]{2,1,0:T(8,128)(2,1)} %bitcast.24), calls=%async_computation.4 | async-start | bytes 262144 | tf_op jit(solution)/shard_map/all_to_all | solution.py:121
  156.4 1.6 bitcast_dynamic-update-slice_fusion.7
  158.0 1.6 fusion.26
  159.6 5.9 %all-to-all-done.4 = bf16[8,32,256]{2,1,0:T(8,128)(2,1)S(1)} async-done(((bf16[8,32,256]{2,1,0:T(8,128)(2,1)}), bf16[8,32,256]{2,1,0:T(8,128)(2,1)S(1)}, u32[]{:S(2)}, u32[]{:S(2)}) %all-to-all-start.4) | async-done | bytes 131104 | tf_op jit(solution)/shard_map/all_to_all | solution.py:121
  166.2 3.4 %all-to-all-start.5 = ((bf16[8,32,256]{2,1,0:T(8,128)(2,1)}), bf16[8,32,256]{2,1,0:T(8,128)(2,1)S(1)}, u32[]{:S(2)}, u32[]{:S(2)}) async-start(bf16[8,32,256]{2,1,0:T(8,128)(2,1)} %broadcast_in_dim.8), calls=%async_computation.5 | async-start | bytes 262144 | tf_op jit(solution)/shard_map/all_to_all | solution.py:20
  169.5 2.3 fusion.32
  171.9 6.6 %all-to-all-done.5 = bf16[8,32,256]{2,1,0:T(8,128)(2,1)S(1)} async-done(((bf16[8,32,256]{2,1,0:T(8,128)(2,1)}), bf16[8,32,256]{2,1,0:T(8,128)(2,1)S(1)}, u32[]{:S(2)}, u32[]{:S(2)}) %all-to-all-start.5) | async-done | bytes 131104 | tf_op jit(solution)/shard_map/all_to_all | solution.py:20
  179.4 1.8 copy.26
  181.2 1.7 fusion.28.a_ref
  182.9 25.0 %shard_map.47 = f32[256,256]{1,0:T(8,128)} custom-call(f32[256,256]{1,0:T(8,128)} %fusion.28.a_ref), custom_call_target="tpu_custom_call" | custom-call | tf_op jit(solution)/shard_map/pallas_call | solution.py:168
  207.9 1.2 fusion.30
  209.1 1.5 fusion.31
  211.1 2.3 fusion.1
  213.9 3.8 %collective-permute-start.9 = (bf16[512,128]{1,0:T(8,128)(2,1)S(1)}, bf16[512,128]{1,0:T(8,128)(2,1)S(1)}, u32[]{:S(2)}, u32[]{:S(2)}) collective-permute-start(bf16[512,128]{1,0:T(8,128)(2,1)S(1)} %get-tuple-element.12), channel_id=1, source_target_pairs={{0,7},{1,0},{2,1},{3,2},{4,3},{5,4},{6,5},{7,6},{8,15},{9,8},{10,9... | collective-permute-start | bytes 393224 | tf_op jit(solution)/shard_map/ppermute | solution.py:98
  217.7 1.7 collective-permute-start.10
  219.7 4.6 %collective-permute-start.12 = (bf16[512,128]{1,0:T(8,128)(2,1)S(1)}, bf16[512,128]{1,0:T(8,128)(2,1)S(1)}, u32[]{:S(2)}, u32[]{:S(2)}) collective-permute-start(bf16[512,128]{1,0:T(8,128)(2,1)S(1)} %get-tuple-element.9), channel_id=1, source_target_pairs={{0,4},{1,5},{2,6},{3,7},{4,0},{5,1},{6,2},{7,3},{8,12},{9,13},{10,... | collective-permute-start | bytes 393224 | tf_op jit(solution)/shard_map/ppermute | solution.py:98
  225.3 4.4 %collective-permute-start.15 = (bf16[512,128]{1,0:T(8,128)(2,1)S(1)}, bf16[512,128]{1,0:T(8,128)(2,1)S(1)}, u32[]{:S(2)}, u32[]{:S(2)}) collective-permute-start(bf16[512,128]{1,0:T(8,128)(2,1)S(1)} %get-tuple-element.6), channel_id=1, source_target_pairs={{0,1},{1,2},{2,3},{3,4},{4,5},{5,6},{6,7},{7,0},{8,9},{9,10},{10,1... | collective-permute-start | bytes 393224 | tf_op jit(solution)/shard_map/ppermute | solution.py:98
  231.0 2.3 collective-permute-done.13
  233.5 2.4 %collective-permute-done.15 = bf16[512,128]{1,0:T(8,128)(2,1)S(1)} collective-permute-done((bf16[512,128]{1,0:T(8,128)(2,1)S(1)}, bf16[512,128]{1,0:T(8,128)(2,1)S(1)}, u32[]{:S(2)}, u32[]{:S(2)}) %collective-permute-start.15) | collective-permute-done | bytes 131104 | tf_op jit(solution)/shard_map/ppermute | solution.py:98
  235.9 1.4 fusion.24
  (58 shorter events, 13.1 us)
Async XLA Ops:
  0.0 6.0 %copy-start = (bf16[1,4096,256]{2,1,0:T(8,128)(2,1)S(1)}, bf16[1,4096,256]{2,1,0:T(8,128)(2,1)}, u32[]{:S(2)}) copy-start(bf16[1,4096,256]{2,1,0:T(8,128)(2,1)} %param.8) | copy-start | bytes 6291460
  0.0 6.0 %copy-start.3 = (bf16[1,512,4096]{2,1,0:T(8,128)(2,1)S(1)}, bf16[1,512,4096]{2,1,0:T(8,128)(2,1)}, u32[]{:S(2)}) copy-start(bf16[1,512,4096]{2,1,0:T(8,128)(2,1)} %param.6) | copy-start | bytes 12582916
  6.0 1.3 copy-start.5
  60.2 31.5 %all-to-all-start.2 = ((bf16[16,128,256]{2,1,0:T(8,128)(2,1)}), bf16[16,128,256]{2,1,0:T(8,128)(2,1)S(1)}, u32[]{:S(2)}, u32[]{:S(2)}) async-start(bf16[16,128,256]{2,1,0:T(8,128)(2,1)} %broadcast_in_dim.6), calls=%async_computation.2 | async-start | bytes 2097152 | tf_op jit(solution)/shard_map/all_to_all | solution.py:20
  68.4 9.9 %collective-permute-start = (bf16[512,128]{1,0:T(8,128)(2,1)}, bf16[512,128]{1,0:T(8,128)(2,1)}, u32[]{:S(2)}, u32[]{:S(2)}) collective-permute-start(bf16[512,128]{1,0:T(8,128)(2,1)} %get-tuple-element.20), channel_id=1, source_target_pairs={{0,7},{1,0},{2,1},{3,2},{4,3},{5,4},{6,5},{7,6},{8,15},{9,8},{10,9... | collective-permute-start | bytes 393224 | tf_op jit(solution)/shard_map/ppermute | solution.py:98
  73.0 8.6 %collective-permute-start.1 = (bf16[512,128]{1,0:T(8,128)(2,1)}, bf16[512,128]{1,0:T(8,128)(2,1)}, u32[]{:S(2)}, u32[]{:S(2)}) collective-permute-start(bf16[512,128]{1,0:T(8,128)(2,1)} %get-tuple-element.19), channel_id=1, source_target_pairs={{0,6},{1,7},{2,0},{3,1},{4,2},{5,3},{6,4},{7,5},{8,14},{9,15},{10,... | collective-permute-start | bytes 393224 | tf_op jit(solution)/shard_map/ppermute | solution.py:98
  73.7 13.8 %collective-permute-start.2 = (bf16[512,128]{1,0:T(8,128)(2,1)}, bf16[512,128]{1,0:T(8,128)(2,1)}, u32[]{:S(2)}, u32[]{:S(2)}) collective-permute-start(bf16[512,128]{1,0:T(8,128)(2,1)} %get-tuple-element.18), channel_id=1, source_target_pairs={{0,5},{1,6},{2,7},{3,0},{4,1},{5,2},{6,3},{7,4},{8,13},{9,14},{10,... | collective-permute-start | bytes 393224 | tf_op jit(solution)/shard_map/ppermute | solution.py:98
  74.9 14.1 %collective-permute-start.3 = (bf16[512,128]{1,0:T(8,128)(2,1)}, bf16[512,128]{1,0:T(8,128)(2,1)}, u32[]{:S(2)}, u32[]{:S(2)}) collective-permute-start(bf16[512,128]{1,0:T(8,128)(2,1)} %get-tuple-element.17), channel_id=1, source_target_pairs={{0,4},{1,5},{2,6},{3,7},{4,0},{5,1},{6,2},{7,3},{8,12},{9,13},{10,... | collective-permute-start | bytes 393224 | tf_op jit(solution)/shard_map/ppermute | solution.py:98
  77.9 65.0 %collective-permute-start.4 = (bf16[512,128]{1,0:T(8,128)(2,1)S(1)}, bf16[512,128]{1,0:T(8,128)(2,1)}, u32[]{:S(2)}, u32[]{:S(2)}) collective-permute-start(bf16[512,128]{1,0:T(8,128)(2,1)S(1)} %get-tuple-element.16), channel_id=1, source_target_pairs={{0,3},{1,4},{2,5},{3,6},{4,7},{5,0},{6,1},{7,2},{8,11},{9,12},{10,... | collective-permute-start | bytes 393224 | tf_op jit(solution)/shard_map/ppermute | solution.py:98
  78.3 67.8 %collective-permute-start.5 = (bf16[512,128]{1,0:T(8,128)(2,1)S(1)}, bf16[512,128]{1,0:T(8,128)(2,1)}, u32[]{:S(2)}, u32[]{:S(2)}) collective-permute-start(bf16[512,128]{1,0:T(8,128)(2,1)S(1)} %get-tuple-element.15), channel_id=1, source_target_pairs={{0,2},{1,3},{2,4},{3,5},{4,6},{5,7},{6,0},{7,1},{8,10},{9,11},{10,... | collective-permute-start | bytes 393224 | tf_op jit(solution)/shard_map/ppermute | solution.py:98
  81.6 74.8 %collective-permute-start.6 = (bf16[512,128]{1,0:T(8,128)(2,1)S(1)}, bf16[512,128]{1,0:T(8,128)(2,1)}, u32[]{:S(2)}, u32[]{:S(2)}) collective-permute-start(bf16[512,128]{1,0:T(8,128)(2,1)S(1)} %get-tuple-element.14), channel_id=1, source_target_pairs={{0,1},{1,2},{2,3},{3,4},{4,5},{5,6},{6,7},{7,0},{8,9},{9,10},{10,1... | collective-permute-start | bytes 393224 | tf_op jit(solution)/shard_map/ppermute | solution.py:98
  97.4 1.3 copy-start.1
  125.3 4.9 %copy-start.4 = (bf16[1,512,4096]{2,1,0:T(8,128)(2,1)S(1)}, bf16[1,512,4096]{2,1,0:T(8,128)(2,1)}, u32[]{:S(2)}) copy-start(bf16[1,512,4096]{2,1,0:T(8,128)(2,1)} %param.6) | copy-start | bytes 12582916
  128.9 1.3 copy-start.2
  130.3 11.8 %copy-start.6 = (bf16[512,512]{1,0:T(8,128)(2,1)S(1)}, bf16[512,512]{1,0:T(8,128)(2,1)}, u32[]{:S(2)}) copy-start(bf16[512,512]{1,0:T(8,128)(2,1)} %copy-done.5) | copy-start | bytes 1572868
  142.7 1.8 collective-permute-start.7
  144.5 5.9 %collective-permute-start.8 = (bf16[256,256]{1,0:T(8,128)(2,1)S(1)}, bf16[256,256]{1,0:T(8,128)(2,1)S(1)}, u32[]{:S(2)}, u32[]{:S(2)}) collective-permute-start(bf16[256,256]{1,0:T(8,128)(2,1)S(1)} %add_convert_fusion.1), channel_id=1, source_target_pairs={{0,128},{8,136},{16,144},{24,152},{32,160},{40,168},{48,176},{56,1... | collective-permute-start | bytes 393224 | tf_op jit(solution)/shard_map/ppermute | solution.py:92
  151.1 14.4 %all-to-all-start.4 = ((bf16[8,32,256]{2,1,0:T(8,128)(2,1)}), bf16[8,32,256]{2,1,0:T(8,128)(2,1)S(1)}, u32[]{:S(2)}, u32[]{:S(2)}) async-start(bf16[8,32,256]{2,1,0:T(8,128)(2,1)} %bitcast.24), calls=%async_computation.4 | async-start | bytes 262144 | tf_op jit(solution)/shard_map/all_to_all | solution.py:121
  166.2 12.4 %all-to-all-start.5 = ((bf16[8,32,256]{2,1,0:T(8,128)(2,1)}), bf16[8,32,256]{2,1,0:T(8,128)(2,1)S(1)}, u32[]{:S(2)}, u32[]{:S(2)}) async-start(bf16[8,32,256]{2,1,0:T(8,128)(2,1)} %broadcast_in_dim.8), calls=%async_computation.5 | async-start | bytes 262144 | tf_op jit(solution)/shard_map/all_to_all | solution.py:20
  213.9 10.4 %collective-permute-start.9 = (bf16[512,128]{1,0:T(8,128)(2,1)S(1)}, bf16[512,128]{1,0:T(8,128)(2,1)S(1)}, u32[]{:S(2)}, u32[]{:S(2)}) collective-permute-start(bf16[512,128]{1,0:T(8,128)(2,1)S(1)} %get-tuple-element.12), channel_id=1, source_target_pairs={{0,7},{1,0},{2,1},{3,2},{4,3},{5,4},{6,5},{7,6},{8,15},{9,8},{10,9... | collective-permute-start | bytes 393224 | tf_op jit(solution)/shard_map/ppermute | solution.py:98
  217.7 7.6 %collective-permute-start.10 = (bf16[512,128]{1,0:T(8,128)(2,1)S(1)}, bf16[512,128]{1,0:T(8,128)(2,1)S(1)}, u32[]{:S(2)}, u32[]{:S(2)}) collective-permute-start(bf16[512,128]{1,0:T(8,128)(2,1)S(1)} %get-tuple-element.11), channel_id=1, source_target_pairs={{0,6},{1,7},{2,0},{3,1},{4,2},{5,3},{6,4},{7,5},{8,14},{9,15},{10,... | collective-permute-start | bytes 393224 | tf_op jit(solution)/shard_map/ppermute | solution.py:98
  219.4 10.4 %collective-permute-start.11 = (bf16[512,128]{1,0:T(8,128)(2,1)S(1)}, bf16[512,128]{1,0:T(8,128)(2,1)S(1)}, u32[]{:S(2)}, u32[]{:S(2)}) collective-permute-start(bf16[512,128]{1,0:T(8,128)(2,1)S(1)} %get-tuple-element.10), channel_id=1, source_target_pairs={{0,5},{1,6},{2,7},{3,0},{4,1},{5,2},{6,3},{7,4},{8,13},{9,14},{10,... | collective-permute-start | bytes 393224 | tf_op jit(solution)/shard_map/ppermute | solution.py:98
  219.7 11.3 %collective-permute-start.12 = (bf16[512,128]{1,0:T(8,128)(2,1)S(1)}, bf16[512,128]{1,0:T(8,128)(2,1)S(1)}, u32[]{:S(2)}, u32[]{:S(2)}) collective-permute-start(bf16[512,128]{1,0:T(8,128)(2,1)S(1)} %get-tuple-element.9), channel_id=1, source_target_pairs={{0,4},{1,5},{2,6},{3,7},{4,0},{5,1},{6,2},{7,3},{8,12},{9,13},{10,... | collective-permute-start | bytes 393224 | tf_op jit(solution)/shard_map/ppermute | solution.py:98
  224.3 9.0 %collective-permute-start.13 = (bf16[512,128]{1,0:T(8,128)(2,1)S(1)}, bf16[512,128]{1,0:T(8,128)(2,1)S(1)}, u32[]{:S(2)}, u32[]{:S(2)}) collective-permute-start(bf16[512,128]{1,0:T(8,128)(2,1)S(1)} %get-tuple-element.8), channel_id=1, source_target_pairs={{0,3},{1,4},{2,5},{3,6},{4,7},{5,0},{6,1},{7,2},{8,11},{9,12},{10,... | collective-permute-start | bytes 393224 | tf_op jit(solution)/shard_map/ppermute | solution.py:98
  224.3 9.1 %collective-permute-start.14 = (bf16[512,128]{1,0:T(8,128)(2,1)S(1)}, bf16[512,128]{1,0:T(8,128)(2,1)S(1)}, u32[]{:S(2)}, u32[]{:S(2)}) collective-permute-start(bf16[512,128]{1,0:T(8,128)(2,1)S(1)} %get-tuple-element.7), channel_id=1, source_target_pairs={{0,2},{1,3},{2,4},{3,5},{4,6},{5,7},{6,0},{7,1},{8,10},{9,11},{10,... | collective-permute-start | bytes 393224 | tf_op jit(solution)/shard_map/ppermute | solution.py:98
  225.3 10.5 %collective-permute-start.15 = (bf16[512,128]{1,0:T(8,128)(2,1)S(1)}, bf16[512,128]{1,0:T(8,128)(2,1)S(1)}, u32[]{:S(2)}, u32[]{:S(2)}) collective-permute-start(bf16[512,128]{1,0:T(8,128)(2,1)S(1)} %get-tuple-element.6), channel_id=1, source_target_pairs={{0,1},{1,2},{2,3},{3,4},{4,5},{5,6},{6,7},{7,0},{8,9},{9,10},{10,1... | collective-permute-start | bytes 393224 | tf_op jit(solution)/shard_map/ppermute | solution.py:98

commit v4 on v3

--- a/solution.py
+++ b/solution.py
@@ -195,8 +195,11 @@
         )
         * scale
     )
-    sketch = chip_first_sum(sketch_term, ("dp_0", "dp_1"), "dp_2").astype(jnp.float32)
-    basis = cholesky_pass(sketch, inner_gram(sketch)).astype(jnp.bfloat16)
+    arrived = chip_first_sum(sketch_term, ("dp_0", "dp_1"), "dp_2")
+    gram = lax.dot_general(
+        arrived, arrived, (((0,), (0,)), ((), ())), preferred_element_type=jnp.float32
+    )
+    basis = cholesky_pass(arrived.astype(jnp.float32), gram).astype(jnp.bfloat16)
     reduced = jnp.dot(features, basis, preferred_element_type=jnp.float32).astype(jnp.bfloat16)
     shaped = jnp.dot(token_gram, reduced, preferred_element_type=jnp.float32).astype(jnp.bfloat16)
     core_term = (

time: 242 us -> 242 us (level)
  no operation moved by 1% of the time
where the time goes in v4:
time: 242 us; the launch traced here: 237 us
  Pallas kernels  50.1 us (21%)
  starting transfers between devices  47.8 us (20%)
  blocking collectives  47.6 us (20%)
  matrix products  37 us (15%)
  waiting for transfers between devices  22.5 us (9%)
  local copies, waits for them, and re-layouts  20.8 us (9%)
  other arithmetic  11.2 us (5%)
    pallas_call x2, Pallas kernels, inverse_factor(): pl.pallas_call(functools.partial(_factor_kernel, panel_rows=64), out_shap...  50.1 us
    all_to_all x1, blocking collectives, chip_first_sum(): lax.all_to_all(blocks, far, split_axis=0, concat_axis=0, tiled=True)  35.9 us
    ppermute x14, starting transfers between devices, shifted(): return lax.ppermute(x, axis, [(j, (j + s) % n) for j in range(n)])  31.7 us
    unnamed x26, local copies, waits for them, and re-layouts  12.2 us
    dot_general x1, matrix products, shards(): jnp.dot(features, basis, preferred_element_type=jnp.float32)  11.8 us
    all_to_all x2, starting transfers between devices, copy_for_each(): lax.all_to_all(jnp.broadcast_to(x[None], (devices, *x.shape)), axis, 0, 0...  9.02 us
    all_to_all x2, waiting for transfers between devices, copy_for_each(): lax.all_to_all(jnp.broadcast_to(x[None], (devices, *x.shape)), axis, 0, 0...  7.77 us
    dot_general x3, matrix products, mm(): return jnp.dot(a, b, precision=lax.Precision.HIGHEST)  6.35 us
  transfers between devices with their start and end apart: 19, of which 9 were waited for; matrix products, arithmetic and copies ran while one was open for 15% of the time, Pallas kernels for 11%

profile of v4, /device:TPU:2, one launch (start us, length us, event | category | flops | bytes accessed | tf_op | source)
XLA Modules:
  0.0 237.4 jit_solution(1876600304063410560)
XLA Ops:
  0.0 6.0 %fusion.10 = bf16[512,512]{1,0:T(8,128)(2,1)S(1)} fusion(bf16[1,512,4096]{2,1,0:T(8,128)(2,1)} %param.7), kind=kOutput, calls=%fused_computation.22 | convolution fusion | flops 2147745792 | bytes 4718592 | tf_op jit(solution)/shard_map/dot_general | solution.py:186
  6.0 1.3 fusion.13
  7.3 5.3 %fusion = bf16[256,4096]{1,0:T(8,128)(2,1)} fusion(bf16[1,512,4096]{2,1,0:T(8,128)(2,1)} %param.6, bf16[512,512]{1,0:T(8,128)(2,1)S(1)} %fusion.10, bf16[512,256]{1,0:T(8,128)(2,1)S(1)} %fusion.13), kind=kOutput, calls=%fused_computation.1 | convolution fusion | flops 1210187776 | bytes 7077888 | tf_op jit(solution)/shard_map/dot_general | solution.py:193
  12.6 1.7 copy.35
  14.3 6.3 %all_to_all.30 = bf16[2,2048,256]{1,2,0:T(8,128)(2,1)} all-to-all(bf16[2,2048,256]{1,2,0:T(8,128)(2,1)S(1)} %bitcast.127), channel_id=1, replica_groups=mesh['dp_0'=2,'dp_1'=8,'dp_2'=2,'blk'=8] {'dp_2'}, dimensions={0} | all-to-all | bytes 4194304 | tf_op jit(solution)/shard_map/all_to_all | solution.py:65
  20.6 2.1 reduce_sum.36
  23.0 35.9 %all_to_all.31 = bf16[16,128,256]{1,2,0:T(8,128)(2,1)S(1)} all-to-all(bf16[16,128,256]{1,2,0:T(8,128)(2,1)S(1)} %copy_bitcast_fusion.1), channel_id=1, replica_groups=mesh['dp_0'=2,'dp_1'=8,'dp_2'=2,'blk'=8] {'dp_0','dp_1'}, dimensions={0} | all-to-all | bytes 2097152 | tf_op jit(solution)/shard_map/all_to_all | solution.py:68
  60.2 5.6 %all-to-all-start.2 = ((bf16[16,128,256]{2,1,0:T(8,128)(2,1)}), bf16[16,128,256]{2,1,0:T(8,128)(2,1)S(1)}, u32[]{:S(2)}, u32[]{:S(2)}) async-start(bf16[16,128,256]{2,1,0:T(8,128)(2,1)} %broadcast_in_dim.6), calls=%async_computation.2 | async-start | bytes 2097152 | tf_op jit(solution)/shard_map/all_to_all | solution.py:20
  65.9 1.6 fusion.27
  68.4 4.6 %collective-permute-start = (bf16[512,128]{1,0:T(8,128)(2,1)}, bf16[512,128]{1,0:T(8,128)(2,1)}, u32[]{:S(2)}, u32[]{:S(2)}) collective-permute-start(bf16[512,128]{1,0:T(8,128)(2,1)} %get-tuple-element.20), channel_id=1, source_target_pairs={{0,7},{1,0},{2,1},{3,2},{4,3},{5,4},{6,5},{7,6},{8,15},{9,8},{10,9... | collective-permute-start | bytes 393224 | tf_op jit(solution)/shard_map/ppermute | solution.py:98
  73.7 1.3 collective-permute-start.2
  74.9 2.9 %collective-permute-start.3 = (bf16[512,128]{1,0:T(8,128)(2,1)}, bf16[512,128]{1,0:T(8,128)(2,1)}, u32[]{:S(2)}, u32[]{:S(2)}) collective-permute-start(bf16[512,128]{1,0:T(8,128)(2,1)} %get-tuple-element.17), channel_id=1, source_target_pairs={{0,4},{1,5},{2,6},{3,7},{4,0},{5,1},{6,2},{7,3},{8,12},{9,13},{10,... | collective-permute-start | bytes 393224 | tf_op jit(solution)/shard_map/ppermute | solution.py:98
  78.3 1.7 collective-permute-start.5
  80.0 1.6 bitcast_dynamic-update-slice_fusion.13
  81.6 4.3 %collective-permute-start.6 = (bf16[512,128]{1,0:T(8,128)(2,1)S(1)}, bf16[512,128]{1,0:T(8,128)(2,1)}, u32[]{:S(2)}, u32[]{:S(2)}) collective-permute-start(bf16[512,128]{1,0:T(8,128)(2,1)S(1)} %get-tuple-element.14), channel_id=1, source_target_pairs={{0,1},{1,2},{2,3},{3,4},{4,5},{5,6},{6,7},{7,0},{8,9},{9,10},{10,1... | collective-permute-start | bytes 393224 | tf_op jit(solution)/shard_map/ppermute | solution.py:98
  85.9 1.6 bitcast_dynamic-update-slice_fusion.12
  87.4 1.6 bitcast_dynamic-update-slice_fusion.11
  89.0 1.6 bitcast_dynamic-update-slice_fusion.10
  91.9 5.4 %all_to_all.32 = bf16[2,16,128,256]{3,2,1,0:T(8,128)(2,1)S(1)} all-to-all(bf16[2,16,128,256]{3,2,1,0:T(8,128)(2,1)S(1)} %broadcast_in_dim.7), channel_id=1, replica_groups=mesh['dp_0'=2,'dp_1'=8,'dp_2'=2,'blk'=8] {'dp_2'}, dimensions={0} | all-to-all | bytes 4194304 | tf_op jit(solution)/shard_map/all_to_all | solution.py:20
  97.4 1.3 copy-done.1
  100.3 25.0 %shard_map.46 = f32[256,256]{1,0:T(8,128)} custom-call(f32[256,256]{1,0:T(8,128)} %fusion.29.a_ref), custom_call_target="tpu_custom_call" | custom-call | tf_op jit(solution)/shard_map/pallas_call | solution.py:168
  125.3 3.6 %convolution_convert_fusion = bf16[4096,256]{1,0:T(8,128)(2,1)S(1)} fusion(bf16[4096,256]{1,0:T(8,128)(2,1)} %bitcast.124, f32[256,256]{1,0:T(8,128)} %shard_map.46), kind=kOutput, calls=%fused_computation.2 | convolution fusion | flops 3222274048 | bytes 4456448 | tf_op jit(solution)/shard_map/dot_general | solution.py:132
  128.9 1.3 copy-done.2
  130.3 11.8 %fusion.18 = bf16[256,512]{1,0:T(8,128)(2,1)S(1)} fusion(bf16[4096,256]{1,0:T(8,128)(2,1)S(1)} %convolution_convert_fusion, bf16[1,512,4096]{2,1,0:T(8,128)(2,1)S(1)} %copy-done.4), kind=kOutput, calls=%fused_computation.24 | convolution fusion | flops 1073872896 | bytes 6553600 | tf_op jit(solution)/shard_map/dot_general | solution.py:203
  142.9 1.6 bitcast_dynamic-update-slice_fusion.9
  144.5 1.5 collective-permute-start.8
  146.1 1.6 bitcast_dynamic-update-slice_fusion.8
  147.6 2.8 %collective-permute-done.8 = bf16[256,256]{1,0:T(8,128)(2,1)S(1)} collective-permute-done((bf16[256,256]{1,0:T(8,128)(2,1)S(1)}, bf16[256,256]{1,0:T(8,128)(2,1)S(1)}, u32[]{:S(2)}, u32[]{:S(2)}) %collective-permute-start.8) | collective-permute-done | bytes 131104 | tf_op jit(solution)/shard_map/ppermute | solution.py:92
  151.1 5.3 %all-to-all-start.4 = ((bf16[8,32,256]{2,1,0:T(8,128)(2,1)}), bf16[8,32,256]{2,1,0:T(8,128)(2,1)S(1)}, u32[]{:S(2)}, u32[]{:S(2)}) async-start(bf16[8,32,256]{2,1,0:T(8,128)(2,1)} %bitcast.24), calls=%async_computation.4 | async-start | bytes 262144 | tf_op jit(solution)/shard_map/all_to_all | solution.py:121
  156.4 1.6 bitcast_dynamic-update-slice_fusion.7
  158.0 1.6 fusion.26
  159.6 5.9 %all-to-all-done.4 = bf16[8,32,256]{2,1,0:T(8,128)(2,1)S(1)} async-done(((bf16[8,32,256]{2,1,0:T(8,128)(2,1)}), bf16[8,32,256]{2,1,0:T(8,128)(2,1)S(1)}, u32[]{:S(2)}, u32[]{:S(2)}) %all-to-all-start.4) | async-done | bytes 131104 | tf_op jit(solution)/shard_map/all_to_all | solution.py:121
  166.2 3.4 %all-to-all-start.5 = ((bf16[8,32,256]{2,1,0:T(8,128)(2,1)}), bf16[8,32,256]{2,1,0:T(8,128)(2,1)S(1)}, u32[]{:S(2)}, u32[]{:S(2)}) async-start(bf16[8,32,256]{2,1,0:T(8,128)(2,1)} %broadcast_in_dim.8), calls=%async_computation.5 | async-start | bytes 262144 | tf_op jit(solution)/shard_map/all_to_all | solution.py:20
  169.5 2.3 fusion.32
  171.9 6.6 %all-to-all-done.5 = bf16[8,32,256]{2,1,0:T(8,128)(2,1)S(1)} async-done(((bf16[8,32,256]{2,1,0:T(8,128)(2,1)}), bf16[8,32,256]{2,1,0:T(8,128)(2,1)S(1)}, u32[]{:S(2)}, u32[]{:S(2)}) %all-to-all-start.5) | async-done | bytes 131104 | tf_op jit(solution)/shard_map/all_to_all | solution.py:20
  179.4 1.8 copy.26
  181.2 1.7 fusion.28.a_ref
  182.9 25.0 %shard_map.47 = f32[256,256]{1,0:T(8,128)} custom-call(f32[256,256]{1,0:T(8,128)} %fusion.28.a_ref), custom_call_target="tpu_custom_call" | custom-call | tf_op jit(solution)/shard_map/pallas_call | solution.py:168
  207.9 1.2 fusion.30
  209.1 1.5 fusion.31
  211.1 2.3 fusion.1
  213.9 3.8 %collective-permute-start.9 = (bf16[512,128]{1,0:T(8,128)(2,1)S(1)}, bf16[512,128]{1,0:T(8,128)(2,1)S(1)}, u32[]{:S(2)}, u32[]{:S(2)}) collective-permute-start(bf16[512,128]{1,0:T(8,128)(2,1)S(1)} %get-tuple-element.12), channel_id=1, source_target_pairs={{0,7},{1,0},{2,1},{3,2},{4,3},{5,4},{6,5},{7,6},{8,15},{9,8},{10,9... | collective-permute-start | bytes 393224 | tf_op jit(solution)/shard_map/ppermute | solution.py:98
  217.7 1.7 collective-permute-start.10
  219.7 4.6 %collective-permute-start.12 = (bf16[512,128]{1,0:T(8,128)(2,1)S(1)}, bf16[512,128]{1,0:T(8,128)(2,1)S(1)}, u32[]{:S(2)}, u32[]{:S(2)}) collective-permute-start(bf16[512,128]{1,0:T(8,128)(2,1)S(1)} %get-tuple-element.9), channel_id=1, source_target_pairs={{0,4},{1,5},{2,6},{3,7},{4,0},{5,1},{6,2},{7,3},{8,12},{9,13},{10,... | collective-permute-start | bytes 393224 | tf_op jit(solution)/shard_map/ppermute | solution.py:98
  225.3 4.4 %collective-permute-start.15 = (bf16[512,128]{1,0:T(8,128)(2,1)S(1)}, bf16[512,128]{1,0:T(8,128)(2,1)S(1)}, u32[]{:S(2)}, u32[]{:S(2)}) collective-permute-start(bf16[512,128]{1,0:T(8,128)(2,1)S(1)} %get-tuple-element.6), channel_id=1, source_target_pairs={{0,1},{1,2},{2,3},{3,4},{4,5},{5,6},{6,7},{7,0},{8,9},{9,10},{10,1... | collective-permute-start | bytes 393224 | tf_op jit(solution)/shard_map/ppermute | solution.py:98
  231.0 2.3 collective-permute-done.13
  233.5 2.4 %collective-permute-done.15 = bf16[512,128]{1,0:T(8,128)(2,1)S(1)} collective-permute-done((bf16[512,128]{1,0:T(8,128)(2,1)S(1)}, bf16[512,128]{1,0:T(8,128)(2,1)S(1)}, u32[]{:S(2)}, u32[]{:S(2)}) %collective-permute-start.15) | collective-permute-done | bytes 131104 | tf_op jit(solution)/shard_map/ppermute | solution.py:98
  235.9 1.4 fusion.24
  (58 shorter events, 13.1 us)
Async XLA Ops:
  0.0 6.0 %copy-start = (bf16[1,4096,256]{2,1,0:T(8,128)(2,1)S(1)}, bf16[1,4096,256]{2,1,0:T(8,128)(2,1)}, u32[]{:S(2)}) copy-start(bf16[1,4096,256]{2,1,0:T(8,128)(2,1)} %param.8) | copy-start | bytes 6291460
  0.0 6.0 %copy-start.3 = (bf16[1,512,4096]{2,1,0:T(8,128)(2,1)S(1)}, bf16[1,512,4096]{2,1,0:T(8,128)(2,1)}, u32[]{:S(2)}) copy-start(bf16[1,512,4096]{2,1,0:T(8,128)(2,1)} %param.6) | copy-start | bytes 12582916
  6.0 1.3 copy-start.5
  60.2 31.5 %all-to-all-start.2 = ((bf16[16,128,256]{2,1,0:T(8,128)(2,1)}), bf16[16,128,256]{2,1,0:T(8,128)(2,1)S(1)}, u32[]{:S(2)}, u32[]{:S(2)}) async-start(bf16[16,128,256]{2,1,0:T(8,128)(2,1)} %broadcast_in_dim.6), calls=%async_computation.2 | async-start | bytes 2097152 | tf_op jit(solution)/shard_map/all_to_all | solution.py:20
  68.4 9.9 %collective-permute-start = (bf16[512,128]{1,0:T(8,128)(2,1)}, bf16[512,128]{1,0:T(8,128)(2,1)}, u32[]{:S(2)}, u32[]{:S(2)}) collective-permute-start(bf16[512,128]{1,0:T(8,128)(2,1)} %get-tuple-element.20), channel_id=1, source_target_pairs={{0,7},{1,0},{2,1},{3,2},{4,3},{5,4},{6,5},{7,6},{8,15},{9,8},{10,9... | collective-permute-start | bytes 393224 | tf_op jit(solution)/shard_map/ppermute | solution.py:98
  73.0 8.6 %collective-permute-start.1 = (bf16[512,128]{1,0:T(8,128)(2,1)}, bf16[512,128]{1,0:T(8,128)(2,1)}, u32[]{:S(2)}, u32[]{:S(2)}) collective-permute-start(bf16[512,128]{1,0:T(8,128)(2,1)} %get-tuple-element.19), channel_id=1, source_target_pairs={{0,6},{1,7},{2,0},{3,1},{4,2},{5,3},{6,4},{7,5},{8,14},{9,15},{10,... | collective-permute-start | bytes 393224 | tf_op jit(solution)/shard_map/ppermute | solution.py:98
  73.7 13.8 %collective-permute-start.2 = (bf16[512,128]{1,0:T(8,128)(2,1)}, bf16[512,128]{1,0:T(8,128)(2,1)}, u32[]{:S(2)}, u32[]{:S(2)}) collective-permute-start(bf16[512,128]{1,0:T(8,128)(2,1)} %get-tuple-element.18), channel_id=1, source_target_pairs={{0,5},{1,6},{2,7},{3,0},{4,1},{5,2},{6,3},{7,4},{8,13},{9,14},{10,... | collective-permute-start | bytes 393224 | tf_op jit(solution)/shard_map/ppermute | solution.py:98
  74.9 14.1 %collective-permute-start.3 = (bf16[512,128]{1,0:T(8,128)(2,1)}, bf16[512,128]{1,0:T(8,128)(2,1)}, u32[]{:S(2)}, u32[]{:S(2)}) collective-permute-start(bf16[512,128]{1,0:T(8,128)(2,1)} %get-tuple-element.17), channel_id=1, source_target_pairs={{0,4},{1,5},{2,6},{3,7},{4,0},{5,1},{6,2},{7,3},{8,12},{9,13},{10,... | collective-permute-start | bytes 393224 | tf_op jit(solution)/shard_map/ppermute | solution.py:98
  77.9 65.0 %collective-permute-start.4 = (bf16[512,128]{1,0:T(8,128)(2,1)S(1)}, bf16[512,128]{1,0:T(8,128)(2,1)}, u32[]{:S(2)}, u32[]{:S(2)}) collective-permute-start(bf16[512,128]{1,0:T(8,128)(2,1)S(1)} %get-tuple-element.16), channel_id=1, source_target_pairs={{0,3},{1,4},{2,5},{3,6},{4,7},{5,0},{6,1},{7,2},{8,11},{9,12},{10,... | collective-permute-start | bytes 393224 | tf_op jit(solution)/shard_map/ppermute | solution.py:98
  78.3 67.8 %collective-permute-start.5 = (bf16[512,128]{1,0:T(8,128)(2,1)S(1)}, bf16[512,128]{1,0:T(8,128)(2,1)}, u32[]{:S(2)}, u32[]{:S(2)}) collective-permute-start(bf16[512,128]{1,0:T(8,128)(2,1)S(1)} %get-tuple-element.15), channel_id=1, source_target_pairs={{0,2},{1,3},{2,4},{3,5},{4,6},{5,7},{6,0},{7,1},{8,10},{9,11},{10,... | collective-permute-start | bytes 393224 | tf_op jit(solution)/shard_map/ppermute | solution.py:98
  81.6 74.8 %collective-permute-start.6 = (bf16[512,128]{1,0:T(8,128)(2,1)S(1)}, bf16[512,128]{1,0:T(8,128)(2,1)}, u32[]{:S(2)}, u32[]{:S(2)}) collective-permute-start(bf16[512,128]{1,0:T(8,128)(2,1)S(1)} %get-tuple-element.14), channel_id=1, source_target_pairs={{0,1},{1,2},{2,3},{3,4},{4,5},{5,6},{6,7},{7,0},{8,9},{9,10},{10,1... | collective-permute-start | bytes 393224 | tf_op jit(solution)/shard_map/ppermute | solution.py:98
  97.4 1.3 copy-start.1
  125.3 4.9 %copy-start.4 = (bf16[1,512,4096]{2,1,0:T(8,128)(2,1)S(1)}, bf16[1,512,4096]{2,1,0:T(8,128)(2,1)}, u32[]{:S(2)}) copy-start(bf16[1,512,4096]{2,1,0:T(8,128)(2,1)} %param.6) | copy-start | bytes 12582916
  128.9 1.3 copy-start.2
  130.3 11.8 %copy-start.6 = (bf16[512,512]{1,0:T(8,128)(2,1)S(1)}, bf16[512,512]{1,0:T(8,128)(2,1)}, u32[]{:S(2)}) copy-start(bf16[512,512]{1,0:T(8,128)(2,1)} %copy-done.5) | copy-start | bytes 1572868
  142.7 1.8 collective-permute-start.7
  144.5 5.9 %collective-permute-start.8 = (bf16[256,256]{1,0:T(8,128)(2,1)S(1)}, bf16[256,256]{1,0:T(8,128)(2,1)S(1)}, u32[]{:S(2)}, u32[]{:S(2)}) collective-permute-start(bf16[256,256]{1,0:T(8,128)(2,1)S(1)} %add_convert_fusion.1), channel_id=1, source_target_pairs={{0,128},{8,136},{16,144},{24,152},{32,160},{40,168},{48,176},{56,1... | collective-permute-start | bytes 393224 | tf_op jit(solution)/shard_map/ppermute | solution.py:92
  151.1 14.4 %all-to-all-start.4 = ((bf16[8,32,256]{2,1,0:T(8,128)(2,1)}), bf16[8,32,256]{2,1,0:T(8,128)(2,1)S(1)}, u32[]{:S(2)}, u32[]{:S(2)}) async-start(bf16[8,32,256]{2,1,0:T(8,128)(2,1)} %bitcast.24), calls=%async_computation.4 | async-start | bytes 262144 | tf_op jit(solution)/shard_map/all_to_all | solution.py:121
  166.2 12.4 %all-to-all-start.5 = ((bf16[8,32,256]{2,1,0:T(8,128)(2,1)}), bf16[8,32,256]{2,1,0:T(8,128)(2,1)S(1)}, u32[]{:S(2)}, u32[]{:S(2)}) async-start(bf16[8,32,256]{2,1,0:T(8,128)(2,1)} %broadcast_in_dim.8), calls=%async_computation.5 | async-start | bytes 262144 | tf_op jit(solution)/shard_map/all_to_all | solution.py:20
  213.9 10.4 %collective-permute-start.9 = (bf16[512,128]{1,0:T(8,128)(2,1)S(1)}, bf16[512,128]{1,0:T(8,128)(2,1)S(1)}, u32[]{:S(2)}, u32[]{:S(2)}) collective-permute-start(bf16[512,128]{1,0:T(8,128)(2,1)S(1)} %get-tuple-element.12), channel_id=1, source_target_pairs={{0,7},{1,0},{2,1},{3,2},{4,3},{5,4},{6,5},{7,6},{8,15},{9,8},{10,9... | collective-permute-start | bytes 393224 | tf_op jit(solution)/shard_map/ppermute | solution.py:98
  217.7 7.6 %collective-permute-start.10 = (bf16[512,128]{1,0:T(8,128)(2,1)S(1)}, bf16[512,128]{1,0:T(8,128)(2,1)S(1)}, u32[]{:S(2)}, u32[]{:S(2)}) collective-permute-start(bf16[512,128]{1,0:T(8,128)(2,1)S(1)} %get-tuple-element.11), channel_id=1, source_target_pairs={{0,6},{1,7},{2,0},{3,1},{4,2},{5,3},{6,4},{7,5},{8,14},{9,15},{10,... | collective-permute-start | bytes 393224 | tf_op jit(solution)/shard_map/ppermute | solution.py:98
  219.4 10.4 %collective-permute-start.11 = (bf16[512,128]{1,0:T(8,128)(2,1)S(1)}, bf16[512,128]{1,0:T(8,128)(2,1)S(1)}, u32[]{:S(2)}, u32[]{:S(2)}) collective-permute-start(bf16[512,128]{1,0:T(8,128)(2,1)S(1)} %get-tuple-element.10), channel_id=1, source_target_pairs={{0,5},{1,6},{2,7},{3,0},{4,1},{5,2},{6,3},{7,4},{8,13},{9,14},{10,... | collective-permute-start | bytes 393224 | tf_op jit(solution)/shard_map/ppermute | solution.py:98
  219.7 11.3 %collective-permute-start.12 = (bf16[512,128]{1,0:T(8,128)(2,1)S(1)}, bf16[512,128]{1,0:T(8,128)(2,1)S(1)}, u32[]{:S(2)}, u32[]{:S(2)}) collective-permute-start(bf16[512,128]{1,0:T(8,128)(2,1)S(1)} %get-tuple-element.9), channel_id=1, source_target_pairs={{0,4},{1,5},{2,6},{3,7},{4,0},{5,1},{6,2},{7,3},{8,12},{9,13},{10,... | collective-permute-start | bytes 393224 | tf_op jit(solution)/shard_map/ppermute | solution.py:98
  224.3 9.0 %collective-permute-start.13 = (bf16[512,128]{1,0:T(8,128)(2,1)S(1)}, bf16[512,128]{1,0:T(8,128)(2,1)S(1)}, u32[]{:S(2)}, u32[]{:S(2)}) collective-permute-start(bf16[512,128]{1,0:T(8,128)(2,1)S(1)} %get-tuple-element.8), channel_id=1, source_target_pairs={{0,3},{1,4},{2,5},{3,6},{4,7},{5,0},{6,1},{7,2},{8,11},{9,12},{10,... | collective-permute-start | bytes 393224 | tf_op jit(solution)/shard_map/ppermute | solution.py:98
  224.3 9.1 %collective-permute-start.14 = (bf16[512,128]{1,0:T(8,128)(2,1)S(1)}, bf16[512,128]{1,0:T(8,128)(2,1)S(1)}, u32[]{:S(2)}, u32[]{:S(2)}) collective-permute-start(bf16[512,128]{1,0:T(8,128)(2,1)S(1)} %get-tuple-element.7), channel_id=1, source_target_pairs={{0,2},{1,3},{2,4},{3,5},{4,6},{5,7},{6,0},{7,1},{8,10},{9,11},{10,... | collective-permute-start | bytes 393224 | tf_op jit(solution)/shard_map/ppermute | solution.py:98
  225.3 10.5 %collective-permute-start.15 = (bf16[512,128]{1,0:T(8,128)(2,1)S(1)}, bf16[512,128]{1,0:T(8,128)(2,1)S(1)}, u32[]{:S(2)}, u32[]{:S(2)}) collective-permute-start(bf16[512,128]{1,0:T(8,128)(2,1)S(1)} %get-tuple-element.6), channel_id=1, source_target_pairs={{0,1},{1,2},{2,3},{3,4},{4,5},{5,6},{6,7},{7,0},{8,9},{9,10},{10,1... | collective-permute-start | bytes 393224 | tf_op jit(solution)/shard_map/ppermute | solution.py:98
